TPU v7x, 32 devices: a whole 2x2x4 slice. The times are simulated.
32 devices in a mesh: group: 1, ctx: 16 (over z, y, x), head: 2 (over core).
Axes of the slice: x: 2, y: 2, z: 4, core: 2. Of those that a mesh axis runs over, the one named last changes fastest.
Arguments:
- pair_raw: bfloat16 [4096, 2, 1024], P(('group', 'ctx'), None, 'head'), may hold values from -6 to 6
- value_raw: bfloat16 [4096, 2048], P(('group', 'ctx'), 'head'), may hold values from -6 to 6
- gate_raw: bfloat16 [4096, 2048], P(('group', 'ctx'), 'head'), may hold values from -6 to 6
- write_strength: float32 [4096, 16], P(('group', 'ctx'), 'head'), may hold values from 0.05 to 0.95
- log_decay: float32 [4096, 16], P(('group', 'ctx'), 'head'), may hold values from -2.6 to 0
- segment_ids: int32 [4096], P('group'), may hold values from 0 to 1, never falling along the last dimension, each value on 1 to 3968 neighbouring positions
- pair_filter: float32 [4, 2, 1024], P(None, None, 'head'), may hold values from -3 to 3
- value_filter: float32 [4, 2048], P(None, 'head'), may hold values from -3 to 3
- norm_gain: float32 [128], replicated, may hold values from 0.1 to 1.9
- out_weight: bfloat16 [2048, 2048], P('head'), may hold values from -0.125 to 0.125
- residual: bfloat16 [4096, 2048], P(('group', 'ctx', 'head')), may hold values from -27 to 27
- post_gain: float32 [2048], replicated, may hold values from 0.1 to 1.9
- routes: int32 [4096, 10], P(('group', 'ctx', 'head')), may hold values from 0 to 31, all different within a row; in each aligned block of 128 rows (0 to 127, 128 to 255, ...) at most 50 rows name the same one
- route_weights: float32 [4096, 10], P(('group', 'ctx', 'head')), may hold values from 0.05 to 0.3
- expert_up: bfloat16 [32, 2048, 1024], P(('ctx', 'head')), may hold values from -0.125 to 0.125
- expert_down: bfloat16 [32, 512, 2048], P(('ctx', 'head')), may hold values from -0.25 to 0.25
Outputs:
- layer_out: bfloat16 [4096, 2048], P(('group', 'ctx', 'head'))
Inputs may be any that keep to these rules, and one draw needn't show every extreme that they name: `routes`: in each aligned block of 128 rows (the rows of one device) no expert is named by more than 50 rows; a row names 10 different experts. `segment_ids`: rollout numbers never fall along the slab; a rollout holds 1 to 3968 tokens of the slab.
All inputs are finite; a program needn't handle non-finite values.
Results may differ from a plain program's by a relative error of at most 0.012.
Values may be sent and summed in bfloat16 or wider, within the bound.
No kernel may reach another device: no remote copies, remote signals or barrier semaphores. Data moves between devices by JAX's collectives and lax.ppermute only.
A program may use at most 128 MiB of HBM per device.

v0:
```python
import jax
import jax.numpy as jnp
from jax import lax
from jax.sharding import PartitionSpec as P

D = 2048
DK = 128
DV = 128
BLOCK = 64


HIGHEST = lax.Precision.HIGHEST


def passed_along(block, axis, distance):
    devices = range(lax.axis_size(axis))
    route = [(i - distance, i) for i in devices if i - distance in devices]
    return lax.ppermute(block, axis, route)


def carried_in_2(shard, axis, combine, identity):
    peers, position = (lax.axis_size(axis), lax.axis_index(axis))
    everything = jax.tree.map(
        lambda part, kind: lax.all_gather(part.astype(kind), axis),
        shard,
        (jnp.bfloat16, jnp.bfloat16),
    )
    start = jax.tree.map(
        lambda part, zero: jnp.broadcast_to(jnp.asarray(zero, part.dtype), part.shape),
        shard,
        identity,
    )

    def step(k, before):
        reached = k < position
        new = combine(
            before, jax.tree.map(lambda part, own: part[k].astype(own.dtype), everything, shard)
        )
        return jax.tree.map(lambda a, b: jnp.where(reached, a, b), new, before)

    return lax.fori_loop(0, peers, step, start)


def precise_dot(left, right):
    return jnp.dot(left, right, precision=HIGHEST, preferred_element_type=jnp.float32)


def causal_filter(padded_raw, filter_taps, padded_ids, kernel):
    length = padded_raw.shape[0] - (kernel - 1)
    source = padded_raw.astype(jnp.float32)
    current_ids = padded_ids[kernel - 1 :]
    summed = jnp.zeros((length, padded_raw.shape[1]), jnp.float32)
    for lag_step in range(kernel):
        offset_start = kernel - 1 - lag_step
        shifted = source[offset_start : offset_start + length]
        matching = (padded_ids[offset_start : offset_start + length] == current_ids).astype(
            jnp.float32
        )
        summed = summed + filter_taps[lag_step] * shifted * matching[:, None]
    return jax.nn.silu(summed)


def unit_rows(values_in):
    return values_in / jnp.sqrt(jnp.sum(values_in * values_in, axis=-1, keepdims=True) + 1e-06)


def mixer_inputs(pair_padded, value_padded, pair_filter, value_filter, padded_ids, kernel):
    pair_act = causal_filter(pair_padded, pair_filter.reshape(kernel, -1), padded_ids, kernel)
    length = pair_act.shape[0]
    pair_heads = pair_act.reshape(length, 2, -1, DK)
    queries = unit_rows(pair_heads[:, 0]) * DK ** (-0.5)
    key_rows = unit_rows(pair_heads[:, 1])
    value_rows = causal_filter(value_padded, value_filter, padded_ids, kernel).reshape(
        length, -1, DV
    )
    repeat_factor = value_rows.shape[1] // key_rows.shape[1]
    return (
        jnp.repeat(queries, repeat_factor, axis=1),
        jnp.repeat(key_rows, repeat_factor, axis=1),
        value_rows,
    )


def block_setup(queries, key_rows, value_rows, strength, decay_rows, segment_here, prior_id):
    cumulative = jnp.cumsum(decay_rows)
    row_index = lax.broadcasted_iota(jnp.int32, (BLOCK, BLOCK), 0)
    col_index = lax.broadcasted_iota(jnp.int32, (BLOCK, BLOCK), 1)
    same_segment = segment_here[:, None] == segment_here[None, :]
    causal = (row_index >= col_index) & same_segment
    strictly = (row_index > col_index) & same_segment
    decay_matrix = jnp.where(
        causal, jnp.exp(jnp.where(causal, cumulative[:, None] - cumulative[None, :], 0.0)), 0.0
    )
    carried_in = (segment_here == prior_id).astype(jnp.float32)
    keyed_beta = key_rows * strength[:, None]
    coupling = jnp.where(strictly, precise_dot(keyed_beta, key_rows.T) * decay_matrix, 0.0)
    system = jnp.eye(BLOCK, dtype=jnp.float32) + coupling
    stacked = jnp.concatenate(
        [value_rows * strength[:, None], keyed_beta * (jnp.exp(cumulative) * carried_in)[:, None]],
        axis=1,
    )
    solved = lax.linalg.triangular_solve(
        system, stacked, left_side=True, lower=True, unit_diagonal=True
    )
    targets = solved[:, :DV]
    corrector = solved[:, DV:]
    within = jnp.where(causal, precise_dot(queries, key_rows.T) * decay_matrix, 0.0)
    query_decayed = queries * (jnp.exp(cumulative) * carried_in)[:, None]
    final_log = cumulative[BLOCK - 1]
    weighting = (segment_here == segment_here[BLOCK - 1]).astype(jnp.float32) * jnp.exp(
        final_log - cumulative
    )
    keys_weighted = key_rows * weighting[:, None]
    transition = jnp.exp(final_log) * carried_in[BLOCK - 1] * jnp.eye(
        DK, dtype=jnp.float32
    ) - precise_dot(keys_weighted.T, corrector)
    increment = precise_dot(keys_weighted.T, targets)
    return (within, query_decayed, targets, corrector, transition, increment)


def head_major(array_in, block_count):
    moved = jnp.moveaxis(array_in, 1, 0)
    return moved.reshape((array_in.shape[1], block_count, BLOCK) + array_in.shape[2:])


def block_tables(queries, key_rows, value_rows, strength, decay_rows, padded_ids, kernel):
    length = queries.shape[0]
    block_count = length // BLOCK
    current_ids = padded_ids[kernel - 1 :].reshape(block_count, BLOCK)
    prior_ids = padded_ids[kernel - 2 : kernel - 2 + length : BLOCK]
    per_block = jax.vmap(block_setup, in_axes=(0, 0, 0, 0, 0, 0, 0))
    per_head = jax.vmap(per_block, in_axes=(0, 0, 0, 0, 0, None, None))
    return per_head(
        head_major(queries, block_count),
        head_major(key_rows, block_count),
        head_major(value_rows, block_count),
        head_major(strength, block_count),
        head_major(decay_rows, block_count),
        current_ids,
        prior_ids,
    )


def batched(left, right):
    return jnp.einsum("hij,hjk->hik", left, right, precision=HIGHEST)


def sweep_blocks(block_terms, start_state):
    blocks_first = tuple((jnp.swapaxes(member, 0, 1) for member in block_terms))

    def advance(carry_state, pieces):
        within, query_decayed, targets, corrector, transition, increment = pieces
        fresh_values = targets - batched(corrector, carry_state)
        emitted = batched(query_decayed, carry_state) + batched(within, fresh_values)
        updated = batched(transition, carry_state) + increment
        return (updated, emitted)

    final_state, emitted = lax.scan(advance, start_state, blocks_first)
    return emitted


def tokens_first(emitted):
    heads_count = emitted.shape[1]
    return jnp.transpose(emitted, (0, 2, 1, 3)).reshape(-1, heads_count, emitted.shape[3])


def gate_output(mixed_heads, gate_raw, norm_gain):
    square_mean = jnp.mean(mixed_heads * mixed_heads, axis=-1, keepdims=True)
    gate_values = jax.nn.silu(gate_raw.reshape(mixed_heads.shape).astype(jnp.float32))
    normed = mixed_heads / jnp.sqrt(square_mean + 1e-06) * norm_gain * gate_values
    return normed.astype(jnp.bfloat16).reshape(mixed_heads.shape[0], -1)


def post_norm(hidden, post_gain):
    hidden_full = hidden.astype(jnp.float32)
    square_mean = jnp.mean(hidden_full * hidden_full, axis=-1, keepdims=True)
    return (hidden_full / jnp.sqrt(square_mean + 1e-06) * post_gain).astype(jnp.bfloat16)


def expert_apply_rows(rows_in, up_matrix, down_matrix):
    hidden_units = down_matrix.shape[0]
    gate_up = jnp.dot(rows_in, up_matrix, preferred_element_type=jnp.float32)
    activated = (jax.nn.silu(gate_up[:, :hidden_units]) * gate_up[:, hidden_units:]).astype(
        jnp.bfloat16
    )
    return jnp.dot(activated, down_matrix, preferred_element_type=jnp.float32).astype(jnp.bfloat16)


def expert_apply(arrived, expert_up, expert_down):
    member_rows = arrived[:, 0]
    flattened = member_rows.reshape(-1, member_rows.shape[-1])
    result = expert_apply_rows(flattened, expert_up[0], expert_down[0])
    outputs = [result.reshape(member_rows.shape)]
    return jnp.stack(outputs, axis=1)


def route_slots(routes, experts_all, capacity):
    assigned = routes.reshape(-1)
    expert_ids = jnp.arange(experts_all, dtype=jnp.int32)
    onehot = (assigned[:, None] == expert_ids[None, :]).astype(jnp.int32)
    slot_rank = jnp.sum((jnp.cumsum(onehot, axis=0) - 1) * onehot, axis=1)
    return assigned * capacity + slot_rank


def per_device(
    pair_raw,
    value_raw,
    gate_raw,
    write_strength,
    log_decay,
    segment_ids,
    pair_filter,
    value_filter,
    norm_gain,
    out_weight,
    residual,
    post_gain,
    routes,
    route_weights,
    expert_up,
    expert_down,
):
    local_tokens = pair_raw.shape[0]
    kernel = value_filter.shape[0]
    pair_flat = pair_raw.reshape(local_tokens, -1)
    pair_width = pair_flat.shape[1]
    rim_rows = jnp.concatenate(
        [pair_flat[local_tokens - (kernel - 1) :], value_raw[local_tokens - (kernel - 1) :]], axis=1
    )
    before = passed_along(rim_rows, "ctx", 1)
    first_token = lax.axis_index("ctx") * local_tokens
    padded_ids = jnp.concatenate([jnp.full((kernel - 1,), -1, jnp.int32), segment_ids])
    window_ids = lax.dynamic_slice_in_dim(padded_ids, first_token, local_tokens + kernel - 1)
    pair_padded = jnp.concatenate([before[:, :pair_width], pair_flat])
    value_padded = jnp.concatenate([before[:, pair_width:], value_raw])
    queries, key_rows, value_rows = mixer_inputs(
        pair_padded, value_padded, pair_filter, value_filter, window_ids, kernel
    )
    block_terms = block_tables(
        queries, key_rows, value_rows, write_strength, log_decay, window_ids, kernel
    )
    heads_here = value_rows.shape[1]
    identity_maps = jnp.broadcast_to(jnp.eye(DK, dtype=jnp.float32), (heads_here, DK, DK))
    empty_state = jnp.zeros((heads_here, DK, DV), jnp.float32)

    def fold_block(totals, pieces):
        transition, increment = pieces
        return ((batched(transition, totals[0]), batched(transition, totals[1]) + increment), None)

    whole_pair, unused = lax.scan(
        fold_block,
        (identity_maps, empty_state),
        (jnp.swapaxes(block_terms[4], 0, 1), jnp.swapaxes(block_terms[5], 0, 1)),
    )
    whole_map, whole_shift = whole_pair

    def join_pairs(earlier, later):
        return (batched(later[0], earlier[0]), batched(later[0], earlier[1]) + later[1])

    prefix = carried_in_2((whole_map, whole_shift), "ctx", join_pairs, (identity_maps, empty_state))
    entering = prefix[1]
    emitted = sweep_blocks(block_terms, entering)
    gated_out = gate_output(tokens_first(emitted), gate_raw, norm_gain)
    attention = lax.psum_scatter(
        jnp.dot(gated_out, out_weight, preferred_element_type=jnp.float32).astype(jnp.bfloat16),
        "head",
        scatter_dimension=0,
        tiled=True,
    ).astype(jnp.float32)
    hidden = (residual.astype(jnp.float32) + attention).astype(jnp.bfloat16)
    expert_in = post_norm(hidden, post_gain)
    devices_all = lax.axis_size("ctx") * lax.axis_size("head")
    local_experts = expert_up.shape[0]
    experts_all = devices_all * local_experts
    local_rows = routes.shape[0]
    top_count = routes.shape[1]
    capacity = local_rows * top_count * 5 // (4 * experts_all)
    slot_index = route_slots(routes, experts_all, capacity)
    owners = jnp.arange(local_rows * top_count, dtype=jnp.int32) // top_count + 1
    owner_table = jnp.zeros((experts_all * capacity,), jnp.int32).at[slot_index].set(owners)
    filled = owner_table > 0
    outgoing = jnp.where(
        filled[:, None], expert_in[jnp.maximum(owner_table - 1, 0)], jnp.zeros((), jnp.bfloat16)
    )
    outgoing = outgoing.reshape(devices_all, local_experts, capacity, D)
    answered = expert_apply(
        lax.all_to_all(outgoing, ("ctx", "head"), split_axis=0, concat_axis=0, tiled=True),
        expert_up,
        expert_down,
    )
    returned = lax.all_to_all(answered, ("ctx", "head"), split_axis=0, concat_axis=0, tiled=True)
    result_rows = returned.reshape(-1, D)
    chosen_slots = slot_index.reshape(local_rows, top_count)
    combined = hidden.astype(jnp.float32)
    for column in range(top_count):
        combined = combined + route_weights[:, column : column + 1] * result_rows[
            chosen_slots[:, column]
        ].astype(jnp.float32)
    return combined.astype(jnp.bfloat16)


def solution(mesh):
    return jax.shard_map(
        per_device,
        mesh=mesh,
        in_specs=(
            P(("group", "ctx"), None, "head"),
            P(("group", "ctx"), "head"),
            P(("group", "ctx"), "head"),
            P(("group", "ctx"), "head"),
            P(("group", "ctx"), "head"),
            P("group"),
            P(None, None, "head"),
            P(None, "head"),
            P(),
            P("head", None),
            P(("group", "ctx", "head"), None),
            P(),
            P(("group", "ctx", "head"), None),
            P(("group", "ctx", "head"), None),
            P(("ctx", "head"), None, None),
            P(("ctx", "head"), None, None),
        ),
        out_specs=P(("group", "ctx", "head"), None),
        check_vma=False,
    )
```

profile of v0, /device:TPU:0, one launch (start us, length us, event | category | flops | bytes accessed | tf_op | source)
XLA Modules:
  0.0 924.0 jit_solution(10823575093657929736)
XLA Ops:
  8.1 4.8 collective-permute-start
  21.9 2.9 multiply_bitcast_fusion.1
  24.7 1.7 reshape.270
  29.9 3.1 fusion.63
  33.0 158.7 %custom-call.3 = f32[8,4,1,64,64]{3,4,2,1,0:T(8,128)} custom-call(f32[8,4,1,64,64]{4,3,2,1,0:T(8,128)} %fusion.63), custom_call_target="InvertDiagBlocksLowerTriangular" | custom-call | tf_op jit(solution)/shard_map/vmap(vmap())/triangular_solve | solution.py:102
  192.8 3.1 multiply_bitcast_fusion
  196.0 2.0 fusion.37
  198.0 3.8 convolution_bitcast_fusion
  203.2 4.0 bitcast_subtract_fusion
  208.8 14.7 %while.40 = (s32[]{:T(128)}, f32[8,128,128]{2,1,0:T(8,128)S(1)}, f32[8,128,128]{2,1,0:T(8,128)S(1)}, f32[4,8,128,128]{3,2,1,0:T(8,128)}, f32[4,8,128,128]{3,2,1,0:T(8,128)}, /*index=5*/s32[]{:T(128)}, s32[]{:T(128)}) while((s32[]{:T(128)}, f32[8,128,128]{2,1,0:T(8,128)S(1)}, f32[8,128,128]{2,1,0:T(8,128)S(1)}, ...), condition=%wide.region_3.4_spmd.clone, body=%wide.region_2.3_spmd.clone.sunk | while | flops 402915328 | bytes 5768791 | solution.py:250
  208.9 1.8 convolution_add_fusion.7
  210.8 1.7 fusion.180
  212.6 1.8 convolution_add_fusion.7
  214.5 1.7 fusion.180
  216.3 1.8 convolution_add_fusion.7
  218.2 1.7 fusion.180
  219.9 1.8 convolution_add_fusion.7
  221.8 1.7 fusion.180
  225.7 3.2 slice_bitcast_fusion.1
  228.9 2.9 fusion.50
  231.8 69.1 %all-gather.5.cloned.1.call-done = bf16[128,128,128]{2,1,0:T(8,128)(2,1)} async-done(((bf16[8,128,128]{2,1,0:T(8,128)(2,1)}), bf16[128,128,128]{2,1,0:T(8,128)(2,1)}) %all-gather.5.cloned.1.call-update) | async-done | bytes 4194320 | tf_op jit(solution)/shard_map/all_gather | solution.py:24
  300.9 77.5 %all-gather.7.cloned.1.call-done = bf16[128,128,128]{2,1,0:T(8,128)(2,1)} async-done(((bf16[8,128,128]{2,1,0:T(8,128)(2,1)}), bf16[128,128,128]{2,1,0:T(8,128)(2,1)}) %all-gather.7.cloned.1.call-update) | async-done | bytes 4194320 | tf_op jit(solution)/shard_map/all_gather | solution.py:24
  378.4 25.3 %while.41 = (s32[]{:T(128)}, f32[8,128,128]{2,1,0:T(8,128)S(1)}, s32[]{:T(128)}, bf16[16,8,128,128]{3,2,1,0:T(8,128)(2,1)}, bf16[16,8,128,128]{3,2,1,0:T(8,128)(2,1)}, /*index=5*/s32[]{:T(128)}, s32[]{:T(128)}) while((s32[]{:T(128)}, f32[8,128,128]{2,1,0:T(8,128)S(1)}, s32[]{:T(128)}, bf16[16,8,128,128]{3,2,1,0:T(8,128)(2,1)}, ...), condition=%wide.region_5.6_spmd.clone, body=%wide.region_4.5_spmd.clone.sunk | while | flops 201981952 | bytes 3148383 | solution.py:41
  403.7 28.7 %while.39 = (s32[]{:T(128)}, f32[8,128,128]{2,1,0:T(8,128)S(1)}, f32[4,8,64,128]{3,2,1,0:T(8,128)}, f32[4,8,128,128]{3,2,1,0:T(8,128)}, f32[4,8,128,128]{3,2,1,0...) while((s32[]{:T(128)}, f32[8,128,128]{2,1,0:T(8,128)S(1)}, ...), condition=%wide.region_8.9_spmd, body=%wide.region_7.8_spmd.sunk | while | flops 453246976 | bytes 6557285 | solution.py:158
  403.7 1.6 convolution_subtract_fusion.2
  406.9 2.1 fusion.175
  409.0 1.8 convolution_add_fusion.6
  410.9 1.6 convolution_subtract_fusion.2
  414.1 2.1 fusion.175
  416.2 1.8 convolution_add_fusion.6
  418.1 1.6 convolution_subtract_fusion.2
  419.7 1.6 fusion.174
  421.3 2.1 fusion.175
  423.3 1.8 convolution_add_fusion.6
  425.2 1.6 convolution_subtract_fusion.2
  428.4 2.1 fusion.175
  430.5 1.8 convolution_add_fusion.6
  432.4 1.6 multiply_reduce_fusion
  434.1 1.8 copy.141
  436.3 4.7 convolution_convert_fusion.1
  441.4 9.1 reduce-window.6
  451.5 5.2 scatter_custom_fusion
  459.6 7.7 gather_fusion
  467.3 8.7 gather.36
  475.9 3.7 select_bitcast_fusion
  479.6 164.2 %all_to_all.10 = bf16[32,1,50,2048]{3,2,1,0:T(8,128)(2,1)} all-to-all(bf16[32,1,50,2048]{3,2,1,0:T(8,128)(2,1)S(1)} %select_bitcast_fusion), channel_id=1, replica_groups=mesh['group'=1,'ctx'=16,'head'=2] {'ctx','head'}, dimensions={0} | all-to-all | bytes 13107200 | tf_op jit(solution)/shard_map/all_to_all | solution.py:287
  643.8 8.8 reshape_squeeze.3
  652.6 10.3 %fusion.34 = f32[1600,1024]{1,0:T(8,128)S(1)} fusion(bf16[1600,2048]{1,0:T(8,128)(2,1)} %reshape_squeeze.3, bf16[1,2048,1024]{2,1,0:T(8,128)(2,1)} %param.36), kind=kOutput, calls=%fused_computation.53 | convolution fusion | flops 6710886400 | bytes 17301504 | tf_op jit(solution)/shard_map/dot_general | solution.py:182
  662.9 5.5 convolution_convert_fusion
  668.4 8.7 stack_reshape.3
  677.1 3.9 all-to-all-start.1
  681.5 162.6 %all-to-all-done.1 = bf16[32,1,50,2048]{3,2,1,0:T(8,128)(2,1)} async-done(((bf16[32,1,50,2048]{3,2,1,0:T(8,128)(2,1)}), bf16[32,1,50,2048]{3,2,1,0:T(8,128)(2,1)}, u32[]{:S(2)}, u32[]{:S(2)}) %all-to-all-start.1) | async-done | bytes 6553632 | tf_op jit(solution)/shard_map/all_to_all | solution.py:291
  844.1 8.9 reshape.279
  853.0 6.0 gather_fusion.1
  859.0 5.9 gather_fusion.2
  864.9 6.0 gather_fusion.3
  870.9 5.9 gather_fusion.4
  876.8 6.0 gather_fusion.5
  882.8 6.0 gather_fusion.6
  888.7 6.2 gather_fusion.7
  894.9 5.9 gather_fusion.8
  900.8 6.0 gather_fusion.9
  906.8 6.0 gather_fusion.10
  912.8 4.5 fusion.82
  (176 shorter events, 54.7 us)
Async XLA Ops:
  6.5 656.3 %copy-start = (bf16[1,512,2048]{2,1,0:T(8,128)(2,1)S(1)}, bf16[1,512,2048]{2,1,0:T(8,128)(2,1)}, u32[]{:S(2)}) copy-start(bf16[1,512,2048]{2,1,0:T(8,128)(2,1)} %param.37) | copy-start | bytes 6291460
  6.5 294.4 %all-gather.5.cloned.1.call-start = ((), (), s32[]{:S(2)}) async-start(), calls=%async_computation.4 | async-start | bytes 4456448 | tf_op jit(solution)/shard_map/all_gather | solution.py:24
  8.1 12.3 %collective-permute-start = (bf16[3,2048]{1,0:T(4,128)(2,1)S(1)}, bf16[3,2048]{1,0:T(4,128)(2,1)S(1)}, u32[]{:S(2)}, u32[]{:S(2)}) collective-permute-start(bf16[3,2048]{1,0:T(4,128)(2,1)S(1)} %pad_maximum_fusion), channel_id=1, source_target_pairs={{0,2},{2,4},{4,6},{6,8},{8,10},{10,12},{12,14},{14,16},{16,18},{18... | collective-permute-start | bytes 36872 | tf_op jit(solution)/shard_map/ppermute | solution.py:18
  26.4 2.4 copy-start.9
  29.9 173.3 %copy-start.1 = (f32[256,4,2,128]{3,0,2,1:T(8,128)}, f32[256,4,2,128]{3,0,2,1:T(8,128)S(1)}, u32[]{:S(2)}) copy-start(f32[256,4,2,128]{3,0,2,1:T(8,128)S(1)} %broadcast_in_dim.52) | copy-start | bytes 3145732
  192.8 3.1 copy-start.5
  192.8 3.1 copy-start.10
  198.0 5.3 copy-start.4
  207.2 1.6 copy-start.3
  208.8 16.8 %copy-start.14 = (f32[128]{0:T(128)S(1)}, f32[128]{0:T(128)}, u32[]{:S(2)}) copy-start(f32[128]{0:T(128)} %param.30) | copy-start | bytes 1540
  224.3 154.0 %all-gather.7.cloned.1.call-start = ((), (), s32[]{:S(2)}) async-start(), calls=%async_computation.5 | async-start | bytes 4456448 | tf_op jit(solution)/shard_map/all_gather | solution.py:24
  225.1 231.8 %reduce-scatter.2.cloned.1.call-start = ((), (), s32[]{:S(2)}) async-start(), calls=%async_computation.3 | async-start | bytes 1572864 | tf_op jit(solution)/shard_map/reduce_scatter | solution.py:264
  225.6 3.3 copy-start.2
  225.6 3.3 copy-start.6
  432.3 3.9 copy-start.15
  436.3 4.7 copy-start.12
  441.0 16.0 %copy-start.7 = (bf16[128,2048]{1,0:T(8,128)(2,1)S(1)}, bf16[128,2048]{1,0:T(8,128)(2,1)}, u32[]{:S(2)}) copy-start(bf16[128,2048]{1,0:T(8,128)(2,1)} %param.32) | copy-start | bytes 1572868
  441.0 17.3 %copy-start.11 = (f32[2048]{0:T(1024)S(1)}, f32[2048]{0:T(1024)}, u32[]{:S(2)}) copy-start(f32[2048]{0:T(1024)} %param.33) | copy-start | bytes 24580
  677.1 4.5 copy-start.13
  677.1 167.1 %all-to-all-start.1 = ((bf16[32,1,50,2048]{3,2,1,0:T(8,128)(2,1)}), bf16[32,1,50,2048]{3,2,1,0:T(8,128)(2,1)}, u32[]{:S(2)}, u32[]{:S(2)}) async-start(bf16[32,1,50,2048]{3,2,1,0:T(8,128)(2,1)} %bitcast.230), calls=%async_computation.2 | async-start | bytes 14680064 | tf_op jit(solution)/shard_map/all_to_all | solution.py:291
  906.8 6.0 copy-start.8
Sparse Core Ops, SparseCore 0:
  224.5 76.3 all-gather.4
  303.7 74.6 all-gather.6
  441.1 7.1 reduce-scatter.1
where the time goes:
time: 932 us; the launch traced here: 924 us
  waiting for transfers between devices  309 us (33%)
  other arithmetic  193 us (21%)
  blocking collectives  164 us (18%)
  local copies, waits for them, and re-layouts  131 us (14%)
  matrix products  103 us (11%)
  between operations  14 us (2%)
    all_to_all x1, blocking collectives, per_device(): lax.all_to_all(outgoing, ('ctx', 'head'), split_axis=0, concat_axis=0, ti...  164 us
    all_to_all x1, waiting for transfers between devices, per_device(): lax.all_to_all(answered, ('ctx', 'head'), split_axis=0, concat_axis=0, ti...  163 us
    another operation x4, other arithmetic, block_setup(): lax.linalg.triangular_solve(system, stacked, left_side=True, lower=True,...  159 us
    all_gather x2, waiting for transfers between devices, carried_in_2(): lax.all_gather(part.astype(kind), axis)  147 us
    dot_general x40, matrix products, batched(): return jnp.einsum('hij,hjk->hik', left, right, precision=HIGHEST)  66.7 us
    gather x10, local copies, waits for them, and re-layouts, per_device(): result_rows[chosen_slots[:, column]].astype(jnp.float32)  59.7 us
  transfers between devices with their start and end apart: 5, of which 3 were waited for; matrix products, arithmetic and copies ran while one was open for 3% of the time, Pallas kernels for 0%

commit v1 on v0

--- a/solution.py
+++ b/solution.py
@@ -18,27 +18,20 @@
     return lax.ppermute(block, axis, route)
 
 
-def carried_in_2(shard, axis, combine, identity):
+def scanned_entry(whole_map, whole_shift, axis):
     peers, position = (lax.axis_size(axis), lax.axis_index(axis))
-    everything = jax.tree.map(
-        lambda part, kind: lax.all_gather(part.astype(kind), axis),
-        shard,
-        (jnp.bfloat16, jnp.bfloat16),
-    )
-    start = jax.tree.map(
-        lambda part, zero: jnp.broadcast_to(jnp.asarray(zero, part.dtype), part.shape),
-        shard,
-        identity,
-    )
-
-    def step(k, before):
-        reached = k < position
-        new = combine(
-            before, jax.tree.map(lambda part, own: part[k].astype(own.dtype), everything, shard)
-        )
-        return jax.tree.map(lambda a, b: jnp.where(reached, a, b), new, before)
-
-    return lax.fori_loop(0, peers, step, start)
+    distance = 1
+    while distance < peers:
+        last = 2 * distance >= peers
+        shift_in = passed_along(whole_shift.astype(jnp.bfloat16), axis, distance).astype(jnp.float32)
+        reached = position >= distance
+        new_shift = batched(whole_map, shift_in) + whole_shift
+        if not last:
+            map_in = passed_along(whole_map.astype(jnp.bfloat16), axis, distance).astype(jnp.float32)
+            whole_map = jnp.where(reached, batched(whole_map, map_in), whole_map)
+        whole_shift = jnp.where(reached, new_shift, whole_shift)
+        distance *= 2
+    return passed_along(whole_shift.astype(jnp.bfloat16), axis, 1).astype(jnp.float32)
 
 
 def precise_dot(left, right):
@@ -81,6 +74,31 @@
     )
 
 
+def unit_lower_inverse(system):
+    size = system.shape[-1]
+    lead = system.shape[:-2]
+    blocks = jnp.ones(lead + (size, 1, 1), system.dtype)
+    width = 1
+    while width < size:
+        count = size // (2 * width)
+        grid = system.reshape(lead + (count, 2 * width, count, 2 * width))
+        diagonal = jnp.moveaxis(jnp.diagonal(grid, axis1=-4, axis2=-2), -1, -3)
+        lower_left = diagonal[..., width:, :width]
+        upper = blocks[..., 0::2, :, :]
+        lower = blocks[..., 1::2, :, :]
+        linked = -jnp.einsum(
+            "...jab,...jbc->...jac",
+            lower,
+            jnp.einsum("...jab,...jbc->...jac", lower_left, upper, precision=HIGHEST),
+            precision=HIGHEST,
+        )
+        top = jnp.concatenate([upper, jnp.zeros_like(upper)], axis=-1)
+        bottom = jnp.concatenate([linked, lower], axis=-1)
+        blocks = jnp.concatenate([top, bottom], axis=-2)
+        width *= 2
+    return blocks.reshape(lead + (size, size))
+
+
 def block_setup(queries, key_rows, value_rows, strength, decay_rows, segment_here, prior_id):
     cumulative = jnp.cumsum(decay_rows)
     row_index = lax.broadcasted_iota(jnp.int32, (BLOCK, BLOCK), 0)
@@ -99,9 +117,7 @@
         [value_rows * strength[:, None], keyed_beta * (jnp.exp(cumulative) * carried_in)[:, None]],
         axis=1,
     )
-    solved = lax.linalg.triangular_solve(
-        system, stacked, left_side=True, lower=True, unit_diagonal=True
-    )
+    solved = precise_dot(unit_lower_inverse(system), stacked)
     targets = solved[:, :DV]
     corrector = solved[:, DV:]
     within = jnp.where(causal, precise_dot(queries, key_rows.T) * decay_matrix, 0.0)
@@ -254,11 +270,7 @@
     )
     whole_map, whole_shift = whole_pair
 
-    def join_pairs(earlier, later):
-        return (batched(later[0], earlier[0]), batched(later[0], earlier[1]) + later[1])
-
-    prefix = carried_in_2((whole_map, whole_shift), "ctx", join_pairs, (identity_maps, empty_state))
-    entering = prefix[1]
+    entering = scanned_entry(whole_map, whole_shift, "ctx")
     emitted = sweep_blocks(block_terms, entering)
     gated_out = gate_output(tokens_first(emitted), gate_raw, norm_gain)
     attention = lax.psum_scatter(
@@ -276,12 +288,13 @@
     top_count = routes.shape[1]
     capacity = local_rows * top_count * 5 // (4 * experts_all)
     slot_index = route_slots(routes, experts_all, capacity)
-    owners = jnp.arange(local_rows * top_count, dtype=jnp.int32) // top_count + 1
-    owner_table = jnp.zeros((experts_all * capacity,), jnp.int32).at[slot_index].set(owners)
-    filled = owner_table > 0
-    outgoing = jnp.where(
-        filled[:, None], expert_in[jnp.maximum(owner_table - 1, 0)], jnp.zeros((), jnp.bfloat16)
-    )
+    chosen_slots = slot_index.reshape(local_rows, top_count)
+    slot_ids = jnp.arange(experts_all * capacity, dtype=jnp.int32)
+    hits = chosen_slots[:, :, None] == slot_ids[None, None, :]
+    picker = jnp.any(hits, axis=1).astype(jnp.bfloat16)
+    outgoing = lax.dot_general(
+        picker, expert_in, (((0,), (0,)), ((), ())), preferred_element_type=jnp.float32
+    ).astype(jnp.bfloat16)
     outgoing = outgoing.reshape(devices_all, local_experts, capacity, D)
     answered = expert_apply(
         lax.all_to_all(outgoing, ("ctx", "head"), split_axis=0, concat_axis=0, tiled=True),
@@ -290,12 +303,13 @@
     )
     returned = lax.all_to_all(answered, ("ctx", "head"), split_axis=0, concat_axis=0, tiled=True)
     result_rows = returned.reshape(-1, D)
-    chosen_slots = slot_index.reshape(local_rows, top_count)
-    combined = hidden.astype(jnp.float32)
-    for column in range(top_count):
-        combined = combined + route_weights[:, column : column + 1] * result_rows[
-            chosen_slots[:, column]
-        ].astype(jnp.float32)
+    weight_table = jnp.sum(jnp.where(hits, route_weights[:, :, None], 0.0), axis=1)
+    weight_high = weight_table.astype(jnp.bfloat16)
+    weight_low = (weight_table - weight_high.astype(jnp.float32)).astype(jnp.bfloat16)
+    routed = jnp.dot(weight_high, result_rows, preferred_element_type=jnp.float32) + jnp.dot(
+        weight_low, result_rows, preferred_element_type=jnp.float32
+    )
+    combined = hidden.astype(jnp.float32) + routed
     return combined.astype(jnp.bfloat16)
 
 

time: 932 us -> 691 us (0.74)
  other arithmetic: 193 us -> 31.5 us
  waiting for transfers between devices: 309 us -> 177 us
  starting transfers between devices: 9.28 us -> 44 us
    another operation x6 -> x2, other arithmetic: 168 us -> 9.11 us  [the longest x4 159 us: block_setup(): lax.linalg.triangular_solve(system, stacked, left_side=True, lower=True,...]
    all_gather x2 -> x0, waiting for transfers between devices: 147 us -> none  [carried_in_2(): lax.all_gather(part.astype(kind), axis)]
    reshape x0 -> x9, local copies, waits for them, and re-layouts: none -> 54.6 us  [the longest x8 46 us: unit_lower_inverse(): grid = system.reshape(lead + (count, 2 * width, count, 2 * width))]
    gather x12 -> x9, local copies, waits for them, and re-layouts: 76.1 us -> 24.5 us  [unit_lower_inverse(): diagonal = jnp.moveaxis(jnp.diagonal(grid, axis1=-4, axis2=-2), -1, -3)]
    ppermute x1 -> x9, starting transfers between devices: 4.84 us -> 40 us  [passed_along(): return lax.ppermute(block, axis, route)]
    dot_general x0 -> x13, matrix products: none -> 30.5 us  [the longest x5 9.36 us: unit_lower_inverse(): jnp.einsum('...jab,...jbc->...jac', lower, jnp.einsum('...jab,...jbc->......]
    dot_general x40 -> x31, matrix products: 66.7 us -> 45.4 us  [batched(): return jnp.einsum('hij,hjk->hik', left, right, precision=HIGHEST)]
  transfers between devices with their start and end apart: 5 -> 11, of which waited for: 3 -> 6; matrix products, arithmetic and copies ran while one was open for 3% -> 4% of each run, Pallas kernels for 0% -> 0%
where the time goes in v1:
time: 691 us; the launch traced here: 683 us
  waiting for transfers between devices  177 us (26%)
  blocking collectives  169 us (24%)
  local copies, waits for them, and re-layouts  135 us (20%)
  matrix products  111 us (16%)
  starting transfers between devices  44 us (6%)
  other arithmetic  31.5 us (5%)
  between operations  14.6 us (2%)
    all_to_all x1, blocking collectives, per_device(): lax.all_to_all(outgoing, ('ctx', 'head'), split_axis=0, concat_axis=0, ti...  169 us
    all_to_all x1, waiting for transfers between devices, per_device(): lax.all_to_all(answered, ('ctx', 'head'), split_axis=0, concat_axis=0, ti...  162 us
    reshape x8, local copies, waits for them, and re-layouts, unit_lower_inverse(): grid = system.reshape(lead + (count, 2 * width, count, 2 * width))  46 us
    dot_general x31, matrix products, batched(): return jnp.einsum('hij,hjk->hik', left, right, precision=HIGHEST)  45.4 us
    ppermute x9, starting transfers between devices, passed_along(): return lax.ppermute(block, axis, route)  40 us
    gather x9, local copies, waits for them, and re-layouts, unit_lower_inverse(): diagonal = jnp.moveaxis(jnp.diagonal(grid, axis1=-4, axis2=-2), -1, -3)  24.5 us
    dot_general x5, matrix products, precise_dot(): jnp.dot(left, right, precision=HIGHEST, preferred_element_type=jnp.float32)  14.8 us
  transfers between devices with their start and end apart: 11, of which 6 were waited for; matrix products, arithmetic and copies ran while one was open for 4% of the time, Pallas kernels for 0%

profile of v1, /device:TPU:0, one launch (start us, length us, event | category | flops | bytes accessed | tf_op | source)
XLA Modules:
  0.0 682.8 jit_solution(16558424283627330187)
XLA Ops:
  8.1 4.8 collective-permute-start
  21.8 2.9 multiply_bitcast_fusion.1
  29.6 2.0 fusion.49
  31.6 4.7 copy.315
  36.3 4.5 reshape.273
  40.9 3.5 reshape.274
  44.3 2.5 reshape.275
  46.8 12.1 %copy.389 = f32[8,4,32,2,32,2]{0,1,4,2,5,3:T(4,128)} copy(f32[8,4,32,2,32,2]{0,5,4,3,2,1:T(2,128)} %bitcast.283) | data formatting | bytes 1048576 | tf_op jit(solution)/shard_map/vmap(vmap())/reshape | solution.py:84
  58.9 4.1 gather_fusion
  66.9 10.7 %copy.388 = f32[8,4,16,4,16,4]{0,5,4,2,3,1:T(4,128)} copy(f32[8,4,16,4,16,4]{0,5,4,3,2,1:T(4,128)} %bitcast.284) | data formatting | bytes 1048576 | tf_op jit(solution)/shard_map/vmap(vmap())/reshape | solution.py:84
  77.7 5.1 gather_fusion.1
  82.7 3.7 copy.321
  86.4 4.8 fusion.110
  91.2 3.7 convolution_negate_fusion.4
  94.9 2.1 select_maximum_fusion.4
  97.0 8.7 %copy.387 = f32[8,4,8,8,8,8]{5,3,4,2,1,0:T(8,128)} copy(f32[8,4,8,8,8,8]{5,4,3,2,1,0:T(8,128)} %reshape.273) | data formatting | bytes 1048576 | tf_op jit(solution)/shard_map/vmap(vmap())/reshape | solution.py:84
  105.7 5.1 gather_fusion.2
  115.2 2.6 convolution_negate_fusion.3
  117.8 2.4 copy.390
  120.2 2.8 gather_fusion.3
  130.4 2.2 gather_fusion.4
  140.3 2.0 fusion.32
  142.3 3.8 convolution_bitcast_fusion
  147.5 4.0 bitcast_subtract_fusion
  153.1 14.7 %while.26 = (s32[]{:T(128)}, f32[8,128,128]{2,1,0:T(8,128)S(1)}, f32[8,128,128]{2,1,0:T(8,128)S(1)}, f32[4,8,128,128]{3,2,1,0:T(8,128)}, f32[4,8,128,128]{3,2,1,0:T(8,128)}, /*index=5*/s32[]{:T(128)}, s32[]{:T(128)}) while((s32[]{:T(128)}, f32[8,128,128]{2,1,0:T(8,128)S(1)}, f32[8,128,128]{2,1,0:T(8,128)S(1)}, ...), condition=%wide.region_3.4_spmd.clone, body=%wide.region_2.3_spmd.clone.sunk | while | flops 402915328 | bytes 5768791 | solution.py:266
  153.1 1.8 convolution_add_fusion.11
  156.8 1.8 convolution_add_fusion.11
  160.5 1.8 convolution_add_fusion.11
  164.2 1.8 convolution_add_fusion.11
  168.6 3.4 collective-permute-start.4
  172.1 3.6 collective-permute-start.1
  175.7 3.3 collective-permute-done.4
  179.4 5.2 collective-permute-start.5
  185.1 4.5 collective-permute-start.2
  191.8 4.8 collective-permute-start.6
  197.0 7.5 %collective-permute-start.3 = (bf16[8,128,128]{2,1,0:T(8,128)(2,1)S(1)}, bf16[8,128,128]{2,1,0:T(8,128)(2,1)S(1)}, u32[]{:S(2)}, u32[]{:S(2)}) collective-permute-start(bf16[8,128,128]{2,1,0:T(8,128)(2,1)S(1)} %get-tuple-element.287), channel_id=1, source_target_pairs={{0,8},{2,10},{4,12},{6,14},{8,16},{10,18},{12,20},{14,22},{16,24},... | collective-permute-start | bytes 786440 | tf_op jit(solution)/shard_map/ppermute | solution.py:18
  204.9 4.6 collective-permute-start.7
  209.6 2.9 fusion.45
  217.1 2.2 collective-permute-done.8
  219.3 28.7 %while.25 = (s32[]{:T(128)}, f32[8,128,128]{2,1,0:T(8,128)S(1)}, f32[4,8,64,128]{3,2,1,0:T(8,128)}, f32[4,8,128,128]{3,2,1,0:T(8,128)}, f32[4,8,128,128]{3,2,1,0...) while((s32[]{:T(128)}, f32[8,128,128]{2,1,0:T(8,128)S(1)}, ...), condition=%wide.region_6.7_spmd, body=%wide.region_5.6_spmd.sunk | while | flops 453246976 | bytes 6557285 | solution.py:174
  222.6 2.1 fusion.205
  224.7 1.8 convolution_add_fusion.10
  229.8 2.1 fusion.205
  231.8 1.8 convolution_add_fusion.10
  237.0 2.1 fusion.205
  239.0 1.8 convolution_add_fusion.10
  244.1 2.0 fusion.205
  246.2 1.8 convolution_add_fusion.10
  249.7 1.8 copy.341
  251.9 4.9 convolution_convert_fusion.2
  257.2 9.1 %reduce-window.6 = s32[32,10,128]{2,1,0:T(8,128)S(1)} reduce-window(s32[32,10,128]{2,1,0:T(8,128)S(1)} %fusion.113, s32[]{:T(128)} %constant.65.clone.1), window={size=1x1x128 pad=0_0x0_0x127_0}, to_apply=%region_9.10 | reduce-window | flops 5201920 | bytes 327684 | tf_op jit(solution)/shard_map/reduce-window
  268.6 6.5 reduce-scatter.2.cloned.1.call-done
  276.4 5.8 convolution_convert_fusion.1
  282.1 8.6 %reshape.286 = bf16[32,1,50,2048]{3,2,0,1:T(8,128)(2,1)} reshape(bf16[1600,2048]{1,0:T(8,128)(2,1)} %convolution_convert_fusion.1) | data formatting | bytes 13107200 | tf_op jit(solution)/shard_map/reshape | solution.py:298
  290.8 169.1 %all_to_all.10 = bf16[32,1,50,2048]{3,2,1,0:T(8,128)(2,1)} all-to-all(bf16[32,1,50,2048]{3,2,1,0:T(8,128)(2,1)} %bitcast.286), channel_id=1, replica_groups=mesh['group'=1,'ctx'=16,'head'=2] {'ctx','head'}, dimensions={0} | all-to-all | bytes 13107200 | tf_op jit(solution)/shard_map/all_to_all | solution.py:300
  459.8 8.8 %reshape_squeeze.3 = bf16[1600,2048]{1,0:T(8,128)(2,1)} reshape(bf16[32,1,50,2048]{3,2,1,0:T(8,128)(2,1)} %all_to_all.10) | data formatting | bytes 13107200 | tf_op jit(solution)/shard_map/reshape;squeeze | solution.py:207
  468.6 10.3 %fusion.27 = f32[1600,1024]{1,0:T(8,128)S(1)} fusion(bf16[1600,2048]{1,0:T(8,128)(2,1)} %reshape_squeeze.3, bf16[1,2048,1024]{2,1,0:T(8,128)(2,1)} %param.34), kind=kOutput, calls=%fused_computation.43 | convolution fusion | flops 6710886400 | bytes 17301504 | tf_op jit(solution)/shard_map/dot_general | solution.py:198
  478.9 5.6 convolution_convert_fusion
  484.5 8.7 %stack_reshape.3 = bf16[32,1,50,2048]{3,2,0,1:T(8,128)(2,1)} reshape(bf16[1600,2048]{1,0:T(8,128)(2,1)} %convolution_convert_fusion) | data formatting | bytes 13107200 | tf_op jit(solution)/shard_map/stack;reshape | solution.py:210
  493.1 4.0 all-to-all-start.1
  498.1 162.2 %all-to-all-done.1 = bf16[32,1,50,2048]{3,2,1,0:T(8,128)(2,1)} async-done(((bf16[32,1,50,2048]{3,2,1,0:T(8,128)(2,1)}), bf16[32,1,50,2048]{3,2,1,0:T(8,128)(2,1)}, u32[]{:S(2)}, u32[]{:S(2)}) %all-to-all-start.1) | async-done | bytes 6553632 | tf_op jit(solution)/shard_map/all_to_all | solution.py:304
  660.2 8.7 %reshape.287 = bf16[1600,2048]{1,0:T(8,128)(2,1)} reshape(bf16[32,1,50,2048]{3,2,1,0:T(8,128)(2,1)} %all-to-all-done.1) | data formatting | bytes 13107200 | tf_op jit(solution)/shard_map/reshape | solution.py:305
  669.0 4.2 fusion.115
  673.7 2.0 fusion.31
  (198 shorter events, 78.0 us)
Async XLA Ops:
  6.5 472.4 %copy-start = (bf16[1,512,2048]{2,1,0:T(8,128)(2,1)S(1)}, bf16[1,512,2048]{2,1,0:T(8,128)(2,1)}, u32[]{:S(2)}) copy-start(bf16[1,512,2048]{2,1,0:T(8,128)(2,1)} %param.35) | copy-start | bytes 6291460
  6.5 268.5 %reduce-scatter.2.cloned.1.call-start = ((), (), s32[]{:S(2)}) async-start(), calls=%async_computation.3 | async-start | bytes 1572864 | tf_op jit(solution)/shard_map/reduce_scatter | solution.py:276
  8.1 12.3 %collective-permute-start = (bf16[3,2048]{1,0:T(4,128)(2,1)S(1)}, bf16[3,2048]{1,0:T(4,128)(2,1)S(1)}, u32[]{:S(2)}, u32[]{:S(2)}) collective-permute-start(bf16[3,2048]{1,0:T(4,128)(2,1)S(1)} %pad_maximum_fusion), channel_id=1, source_target_pairs={{0,2},{2,4},{4,6},{6,8},{8,10},{10,12},{12,14},{14,16},{16,18},{18... | collective-permute-start | bytes 36872 | tf_op jit(solution)/shard_map/ppermute | solution.py:18
  28.6 1.0 copy-start.2
  31.6 12.7 %copy-start.6 = (f32[8,4,64,64]{3,2,1,0:T(8,128)}, f32[8,4,64,64]{3,2,1,0:T(8,128)S(1)}, u32[]{:S(2)}) copy-start(f32[8,4,64,64]{3,2,1,0:T(8,128)S(1)} %fusion.49) | copy-start | bytes 1572868
  46.8 17.7 %copy-start.21 = (f32[32,2]{1,0:T(8,128)S(1)}, f32[32,2]{1,0:T(8,128)}, u32[]{:S(2)}) copy-start(f32[32,2]{1,0:T(8,128)} %constant.115.clone.1) | copy-start | bytes 772
  66.9 19.5 %copy-start.14 = (f32[8,4,16,2,2]{4,3,2,1,0:T(2,128)}, f32[8,4,16,2,2]{4,3,2,1,0:T(2,128)S(1)}, u32[]{:S(2)}) copy-start(f32[8,4,16,2,2]{4,3,2,1,0:T(2,128)S(1)} %get-tuple-element.256) | copy-start | bytes 24580
  66.9 24.3 %copy-start.18 = (f32[8,4,16,2,2]{4,3,2,1,0:T(2,128)}, f32[8,4,16,2,2]{4,3,2,1,0:T(2,128)S(1)}, u32[]{:S(2)}) copy-start(f32[8,4,16,2,2]{4,3,2,1,0:T(2,128)S(1)} %get-tuple-element.255) | copy-start | bytes 24580
  112.1 5.7 copy-start.10
  125.0 3.8 copy-start.13
  135.5 1.2 copy-start.7
  136.5 1.6 copy-start.19
  136.5 1.7 copy-start.17
  137.4 1.3 copy-start.3
  138.3 1.9 copy-start.11
  142.3 5.3 copy-start.8
  151.5 1.5 copy-start.5
  153.1 18.9 %copy-start.24 = (f32[128]{0:T(128)S(1)}, f32[128]{0:T(128)}, u32[]{:S(2)}) copy-start(f32[128]{0:T(128)} %param.28) | copy-start | bytes 1540
  168.6 10.5 %collective-permute-start.4 = (bf16[8,128,128]{2,1,0:T(8,128)(2,1)}, bf16[8,128,128]{2,1,0:T(8,128)(2,1)S(1)}, u32[]{:S(2)}, u32[]{:S(2)}) collective-permute-start(bf16[8,128,128]{2,1,0:T(8,128)(2,1)} %convert_element_type.154), channel_id=1, source_target_pairs={{0,2},{2,4},{4,6},{6,8},{8,10},{10,12},{12,14},{14,16},{16,18},{18... | collective-permute-start | bytes 786440 | tf_op jit(solution)/shard_map/ppermute | solution.py:18
  172.1 12.6 %collective-permute-start.1 = (bf16[8,128,128]{2,1,0:T(8,128)(2,1)S(1)}, bf16[8,128,128]{2,1,0:T(8,128)(2,1)S(1)}, u32[]{:S(2)}, u32[]{:S(2)}) collective-permute-start(bf16[8,128,128]{2,1,0:T(8,128)(2,1)S(1)} %convert_element_type.151), channel_id=1, source_target_pairs={{0,2},{2,4},{4,6},{6,8},{8,10},{10,12},{12,14},{14,16},{16,18},{18... | collective-permute-start | bytes 786440 | tf_op jit(solution)/shard_map/ppermute | solution.py:18
  179.4 12.0 %collective-permute-start.5 = (bf16[8,128,128]{2,1,0:T(8,128)(2,1)S(1)}, bf16[8,128,128]{2,1,0:T(8,128)(2,1)S(1)}, u32[]{:S(2)}, u32[]{:S(2)}) collective-permute-start(bf16[8,128,128]{2,1,0:T(8,128)(2,1)S(1)} %get-tuple-element.281), channel_id=1, source_target_pairs={{0,4},{2,6},{4,8},{6,10},{8,12},{10,14},{12,16},{14,18},{16,20},{1... | collective-permute-start | bytes 786440 | tf_op jit(solution)/shard_map/ppermute | solution.py:18
  185.1 24.5 %copy-start.4 = (f32[256,4,2,128]{3,0,2,1:T(8,128)S(1)}, f32[256,4,2,128]{3,0,2,1:T(8,128)}, u32[]{:S(2)}) copy-start(f32[256,4,2,128]{3,0,2,1:T(8,128)} %copy-done.2) | copy-start | bytes 3145732
  185.1 24.5 %copy-start.12 = (f32[256,4,2,128]{3,0,2,1:T(8,128)S(1)}, f32[256,4,2,128]{3,0,2,1:T(8,128)}, u32[]{:S(2)}) copy-start(f32[256,4,2,128]{3,0,2,1:T(8,128)} %copy-done.11) | copy-start | bytes 3145732
  185.1 11.5 %collective-permute-start.2 = (bf16[8,128,128]{2,1,0:T(8,128)(2,1)S(1)}, bf16[8,128,128]{2,1,0:T(8,128)(2,1)S(1)}, u32[]{:S(2)}, u32[]{:S(2)}) collective-permute-start(bf16[8,128,128]{2,1,0:T(8,128)(2,1)S(1)} %get-tuple-element.283), channel_id=1, source_target_pairs={{0,4},{2,6},{4,8},{6,10},{8,12},{10,14},{12,16},{14,18},{16,20},{1... | collective-permute-start | bytes 786440 | tf_op jit(solution)/shard_map/ppermute | solution.py:18
  191.8 12.7 %collective-permute-start.6 = (bf16[8,128,128]{2,1,0:T(8,128)(2,1)S(1)}, bf16[8,128,128]{2,1,0:T(8,128)(2,1)S(1)}, u32[]{:S(2)}, u32[]{:S(2)}) collective-permute-start(bf16[8,128,128]{2,1,0:T(8,128)(2,1)S(1)} %get-tuple-element.285), channel_id=1, source_target_pairs={{0,8},{2,10},{4,12},{6,14},{8,16},{10,18},{12,20},{14,22},{16,24},... | collective-permute-start | bytes 786440 | tf_op jit(solution)/shard_map/ppermute | solution.py:18
  197.0 15.5 %collective-permute-start.3 = (bf16[8,128,128]{2,1,0:T(8,128)(2,1)S(1)}, bf16[8,128,128]{2,1,0:T(8,128)(2,1)S(1)}, u32[]{:S(2)}, u32[]{:S(2)}) collective-permute-start(bf16[8,128,128]{2,1,0:T(8,128)(2,1)S(1)} %get-tuple-element.287), channel_id=1, source_target_pairs={{0,8},{2,10},{4,12},{6,14},{8,16},{10,18},{12,20},{14,22},{16,24},... | collective-permute-start | bytes 786440 | tf_op jit(solution)/shard_map/ppermute | solution.py:18
  204.9 10.5 %copy-start.9 = (f32[8,4,64,256]{3,2,1,0:T(8,128)S(1)}, f32[8,4,64,256]{3,2,1,0:T(8,128)}, u32[]{:S(2)}) copy-start(f32[8,4,64,256]{3,2,1,0:T(8,128)} %copy-done.8) | copy-start | bytes 6291460
  204.9 8.5 %collective-permute-start.7 = (bf16[8,128,128]{2,1,0:T(8,128)(2,1)S(1)}, bf16[8,128,128]{2,1,0:T(8,128)(2,1)S(1)}, u32[]{:S(2)}, u32[]{:S(2)}) collective-permute-start(bf16[8,128,128]{2,1,0:T(8,128)(2,1)S(1)} %get-tuple-element.289), channel_id=1, source_target_pairs={{0,16},{2,18},{4,20},{6,22},{8,24},{10,26},{12,28},{14,30},{1,17},... | collective-permute-start | bytes 786440 | tf_op jit(solution)/shard_map/ppermute | solution.py:18
  213.9 5.4 collective-permute-start.8
  251.9 4.9 copy-start.20
  256.8 18.3 %copy-start.15 = (bf16[128,2048]{1,0:T(8,128)(2,1)S(1)}, bf16[128,2048]{1,0:T(8,128)(2,1)}, u32[]{:S(2)}) copy-start(bf16[128,2048]{1,0:T(8,128)(2,1)} %param.30) | copy-start | bytes 1572868
  256.8 19.6 %copy-start.23 = (f32[2048]{0:T(1024)S(1)}, f32[2048]{0:T(1024)}, u32[]{:S(2)}) copy-start(f32[2048]{0:T(1024)} %param.31) | copy-start | bytes 24580
  493.1 4.0 copy-start.22
  493.1 167.1 %all-to-all-start.1 = ((bf16[32,1,50,2048]{3,2,1,0:T(8,128)(2,1)}), bf16[32,1,50,2048]{3,2,1,0:T(8,128)(2,1)}, u32[]{:S(2)}, u32[]{:S(2)}) async-start(bf16[32,1,50,2048]{3,2,1,0:T(8,128)(2,1)} %bitcast.285), calls=%async_computation.2 | async-start | bytes 14680064 | tf_op jit(solution)/shard_map/all_to_all | solution.py:304
  668.9 4.7 copy-start.1
  669.0 4.8 copy-start.16
Sparse Core Ops, SparseCore 0:
  256.9 18.0 reduce-scatter.1

commit v2 on v1

--- a/solution.py
+++ b/solution.py
@@ -1,12 +1,13 @@
 import jax
 import jax.numpy as jnp
 from jax import lax
-from jax.sharding import PartitionSpec as P
+from jax.sharding import Mesh, PartitionSpec as P
 
 D = 2048
 DK = 128
 DV = 128
 BLOCK = 64
+CTX = ("ctx_hi", "ctx_lo")
 
 
 HIGHEST = lax.Precision.HIGHEST
@@ -243,8 +244,8 @@
     rim_rows = jnp.concatenate(
         [pair_flat[local_tokens - (kernel - 1) :], value_raw[local_tokens - (kernel - 1) :]], axis=1
     )
-    before = passed_along(rim_rows, "ctx", 1)
-    first_token = lax.axis_index("ctx") * local_tokens
+    before = passed_along(rim_rows, CTX, 1)
+    first_token = lax.axis_index(CTX) * local_tokens
     padded_ids = jnp.concatenate([jnp.full((kernel - 1,), -1, jnp.int32), segment_ids])
     window_ids = lax.dynamic_slice_in_dim(padded_ids, first_token, local_tokens + kernel - 1)
     pair_padded = jnp.concatenate([before[:, :pair_width], pair_flat])
@@ -270,7 +271,7 @@
     )
     whole_map, whole_shift = whole_pair
 
-    entering = scanned_entry(whole_map, whole_shift, "ctx")
+    entering = scanned_entry(whole_map, whole_shift, CTX)
     emitted = sweep_blocks(block_terms, entering)
     gated_out = gate_output(tokens_first(emitted), gate_raw, norm_gain)
     attention = lax.psum_scatter(
@@ -281,60 +282,90 @@
     ).astype(jnp.float32)
     hidden = (residual.astype(jnp.float32) + attention).astype(jnp.bfloat16)
     expert_in = post_norm(hidden, post_gain)
-    devices_all = lax.axis_size("ctx") * lax.axis_size("head")
+    levels = lax.axis_size("ctx_hi")
+    level = lax.axis_index("ctx_hi")
     local_experts = expert_up.shape[0]
-    experts_all = devices_all * local_experts
+    per_level = lax.axis_size("ctx_lo") * lax.axis_size("head") * local_experts
+    experts_all = levels * per_level
     local_rows = routes.shape[0]
     top_count = routes.shape[1]
     capacity = local_rows * top_count * 5 // (4 * experts_all)
-    slot_index = route_slots(routes, experts_all, capacity)
-    chosen_slots = slot_index.reshape(local_rows, top_count)
-    slot_ids = jnp.arange(experts_all * capacity, dtype=jnp.int32)
+    gathered_in = lax.all_gather(expert_in, "ctx_hi").reshape(levels * local_rows, D)
+    gathered_routes = lax.all_gather(routes, "ctx_hi").reshape(levels, local_rows * top_count)
+    gathered_weights = lax.all_gather(route_weights, "ctx_hi").reshape(levels * local_rows, top_count)
+    expert_ids = jnp.arange(experts_all, dtype=jnp.int32)
+    onehot = (gathered_routes[:, :, None] == expert_ids[None, None, :]).astype(jnp.int32)
+    slot_rank = jnp.sum((jnp.cumsum(onehot, axis=1) - 1) * onehot, axis=2)
+    source = lax.broadcasted_iota(jnp.int32, gathered_routes.shape, 0)
+    within = gathered_routes % per_level
+    slot_index = jnp.where(
+        gathered_routes // per_level == level, (within * levels + source) * capacity + slot_rank, -1
+    )
+    slots_total = per_level * levels * capacity
+    chosen_slots = slot_index.reshape(levels * local_rows, top_count)
+    slot_ids = jnp.arange(slots_total, dtype=jnp.int32)
     hits = chosen_slots[:, :, None] == slot_ids[None, None, :]
     picker = jnp.any(hits, axis=1).astype(jnp.bfloat16)
     outgoing = lax.dot_general(
-        picker, expert_in, (((0,), (0,)), ((), ())), preferred_element_type=jnp.float32
+        picker, gathered_in, (((0,), (0,)), ((), ())), preferred_element_type=jnp.float32
     ).astype(jnp.bfloat16)
-    outgoing = outgoing.reshape(devices_all, local_experts, capacity, D)
-    answered = expert_apply(
-        lax.all_to_all(outgoing, ("ctx", "head"), split_axis=0, concat_axis=0, tiled=True),
-        expert_up,
-        expert_down,
-    )
-    returned = lax.all_to_all(answered, ("ctx", "head"), split_axis=0, concat_axis=0, tiled=True)
-    result_rows = returned.reshape(-1, D)
-    weight_table = jnp.sum(jnp.where(hits, route_weights[:, :, None], 0.0), axis=1)
+    level_axes = ("ctx_lo", "head")
+    outgoing = outgoing.reshape(per_level // local_experts, local_experts * levels * capacity, D)
+    arrived = lax.all_to_all(outgoing, level_axes, split_axis=0, concat_axis=0, tiled=True)
+    arrived = arrived.reshape(per_level // local_experts, local_experts, levels * capacity, D)
+    answered = jnp.stack(
+        [
+            expert_apply_rows(
+                arrived[:, member].reshape(-1, D), expert_up[member], expert_down[member]
+            ).reshape(arrived.shape[0], levels * capacity, D)
+            for member in range(local_experts)
+        ],
+        axis=1,
+    ).reshape(per_level // local_experts, local_experts * levels * capacity, D)
+    returned = lax.all_to_all(answered, level_axes, split_axis=0, concat_axis=0, tiled=True)
+    result_rows = returned.reshape(slots_total, D)
+    weight_table = jnp.sum(jnp.where(hits, gathered_weights[:, :, None], 0.0), axis=1)
     weight_high = weight_table.astype(jnp.bfloat16)
     weight_low = (weight_table - weight_high.astype(jnp.float32)).astype(jnp.bfloat16)
-    routed = jnp.dot(weight_high, result_rows, preferred_element_type=jnp.float32) + jnp.dot(
+    partial = jnp.dot(weight_high, result_rows, preferred_element_type=jnp.float32) + jnp.dot(
         weight_low, result_rows, preferred_element_type=jnp.float32
     )
+    routed = lax.psum_scatter(
+        partial.astype(jnp.bfloat16), "ctx_hi", scatter_dimension=0, tiled=True
+    ).astype(jnp.float32)
     combined = hidden.astype(jnp.float32) + routed
     return combined.astype(jnp.bfloat16)
+
+
+def split_mesh(mesh):
+    groups, peers, pairs = (mesh.shape["group"], mesh.shape["ctx"], mesh.shape["head"])
+    low = 4 if peers % 4 == 0 else 1
+    devices = mesh.devices.reshape(groups, peers // low, low, pairs)
+    return Mesh(devices, ("group", "ctx_hi", "ctx_lo", "head"))
 
 
 def solution(mesh):
     return jax.shard_map(
         per_device,
-        mesh=mesh,
+        mesh=split_mesh(mesh),
         in_specs=(
-            P(("group", "ctx"), None, "head"),
-            P(("group", "ctx"), "head"),
-            P(("group", "ctx"), "head"),
-            P(("group", "ctx"), "head"),
-            P(("group", "ctx"), "head"),
+            P(("group", "ctx_hi", "ctx_lo"), None, "head"),
+            P(("group", "ctx_hi", "ctx_lo"), "head"),
+            P(("group", "ctx_hi", "ctx_lo"), "head"),
+            P(("group", "ctx_hi", "ctx_lo"), "head"),
+            P(("group", "ctx_hi", "ctx_lo"), "head"),
             P("group"),
             P(None, None, "head"),
             P(None, "head"),
             P(),
             P("head", None),
-            P(("group", "ctx", "head"), None),
+            P(("group", "ctx_hi", "ctx_lo", "head"), None),
             P(),
-            P(("group", "ctx", "head"), None),
-            P(("group", "ctx", "head"), None),
-            P(("ctx", "head"), None, None),
-            P(("ctx", "head"), None, None),
+            P(("group", "ctx_hi", "ctx_lo", "head"), None),
+            P(("group", "ctx_hi", "ctx_lo", "head"), None),
+            P(("ctx_hi", "ctx_lo", "head"), None, None),
+            P(("ctx_hi", "ctx_lo", "head"), None, None),
         ),
-        out_specs=P(("group", "ctx", "head"), None),
+        out_specs=P(("group", "ctx_hi", "ctx_lo", "head"), None),
         check_vma=False,
     )

time: 691 us -> 628 us (0.909)
  other arithmetic: 31.5 us -> 102 us
  blocking collectives: 169 us -> 107 us
  waiting for transfers between devices: 177 us -> 125 us
  local copies, waits for them, and re-layouts: 135 us -> 104 us
  matrix products: 111 us -> 118 us
    all_to_all x1, waiting for transfers between devices: 162 us -> 54.9 us  [per_device(): lax.all_to_all(answered, level_axes, split_axis=0, concat_axis=0, tiled=T...]
    all_to_all x1, blocking collectives: 169 us -> 78.5 us  [per_device(): lax.all_to_all(outgoing, level_axes, split_axis=0, concat_axis=0, tiled=T...]
    another operation x2, other arithmetic: 9.11 us -> 62.8 us
    reduce_scatter x0 -> x1, waiting for transfers between devices: none -> 43.6 us  [per_device(): lax.psum_scatter(partial.astype(jnp.bfloat16), 'ctx_hi', scatter_dimensio...]
    all_gather x0 -> x2, blocking collectives: none -> 28.8 us  [the longest x1 15.5 us: per_device(): lax.all_gather(routes, 'ctx_hi').reshape(levels, local_rows * top_count)]
    another operation x3 -> x2, local copies, waits for them, and re-layouts: 17.5 us -> 0.11 us  [the longest x1 8.75 us: expert_apply(): flattened = member_rows.reshape(-1, member_rows.shape[-1])]
    reshape x2 -> x0, local copies, waits for them, and re-layouts: 17.4 us -> none  [the longest x1 8.73 us: per_device(): result_rows = returned.reshape(-1, D)]
    reduce_scatter x1, waiting for transfers between devices: 6.47 us -> 18.2 us  [per_device(): lax.psum_scatter(jnp.dot(gated_out, out_weight, preferred_element_type=jn...]
  transfers between devices with their start and end apart: 11 -> 13, of which waited for: 6 -> 7; matrix products, arithmetic and copies ran while one was open for 4% -> 16% of each run, Pallas kernels for 0% -> 0%
where the time goes in v2:
time: 628 us; the launch traced here: 616 us
  waiting for transfers between devices  125 us (20%)
  matrix products  118 us (19%)
  blocking collectives  107 us (17%)
  local copies, waits for them, and re-layouts  104 us (17%)
  other arithmetic  102 us (16%)
  starting transfers between devices  45 us (7%)
  between operations  14.4 us (2%)
    all_to_all x1, blocking collectives, per_device(): lax.all_to_all(outgoing, level_axes, split_axis=0, concat_axis=0, tiled=T...  78.5 us
    another operation x2, other arithmetic  62.8 us
    all_to_all x1, waiting for transfers between devices, per_device(): lax.all_to_all(answered, level_axes, split_axis=0, concat_axis=0, tiled=T...  54.9 us
    reshape x8, local copies, waits for them, and re-layouts, unit_lower_inverse(): grid = system.reshape(lead + (count, 2 * width, count, 2 * width))  46.1 us
    dot_general x31, matrix products, batched(): return jnp.einsum('hij,hjk->hik', left, right, precision=HIGHEST)  45.4 us
    reduce_scatter x1, waiting for transfers between devices, per_device(): lax.psum_scatter(partial.astype(jnp.bfloat16), 'ctx_hi', scatter_dimensio...  43.6 us
    ppermute x9, starting transfers between devices, passed_along(): return lax.ppermute(block, axis, route)  40 us
    gather x9, local copies, waits for them, and re-layouts, unit_lower_inverse(): diagonal = jnp.moveaxis(jnp.diagonal(grid, axis1=-4, axis2=-2), -1, -3)  24.5 us
  transfers between devices with their start and end apart: 13, of which 7 were waited for; matrix products, arithmetic and copies ran while one was open for 16% of the time, Pallas kernels for 0%

profile of v2, /device:TPU:0, one launch (start us, length us, event | category | flops | bytes accessed | tf_op | source)
XLA Modules:
  0.0 615.9 jit_solution(13315210089995124457)
XLA Ops:
  8.1 4.8 collective-permute-start
  21.8 2.9 multiply_bitcast_fusion.1
  29.6 2.0 fusion.47
  31.7 4.7 copy.250
  36.3 4.6 reshape.337
  40.9 3.5 reshape.338
  44.4 2.5 reshape.339
  46.8 12.1 %copy.319 = f32[8,4,32,2,32,2]{0,1,4,2,5,3:T(4,128)} copy(f32[8,4,32,2,32,2]{0,5,4,3,2,1:T(2,128)} %bitcast.280) | data formatting | bytes 1048576 | tf_op jit(solution)/shard_map/vmap(vmap())/reshape | solution.py:85
  59.0 4.1 gather_fusion
  67.0 10.8 %copy.318 = f32[8,4,16,4,16,4]{0,5,4,2,3,1:T(4,128)} copy(f32[8,4,16,4,16,4]{0,5,4,3,2,1:T(4,128)} %bitcast.281) | data formatting | bytes 1048576 | tf_op jit(solution)/shard_map/vmap(vmap())/reshape | solution.py:85
  77.7 5.1 gather_fusion.1
  82.8 3.6 copy.256
  86.5 4.8 fusion.111
  91.2 3.7 convolution_negate_fusion.4
  95.0 2.1 select_maximum_fusion.4
  97.1 8.7 %copy.317 = f32[8,4,8,8,8,8]{5,3,4,2,1,0:T(8,128)} copy(f32[8,4,8,8,8,8]{5,4,3,2,1,0:T(8,128)} %reshape.337) | data formatting | bytes 1048576 | tf_op jit(solution)/shard_map/vmap(vmap())/reshape | solution.py:85
  105.8 5.1 gather_fusion.2
  115.3 2.6 convolution_negate_fusion.3
  117.9 2.4 copy.320
  120.4 2.8 gather_fusion.3
  130.6 2.2 gather_fusion.4
  140.4 2.0 fusion.30
  142.5 3.8 convolution_bitcast_fusion
  147.7 4.0 bitcast_subtract_fusion
  153.3 14.7 %while.26 = (s32[]{:T(128)}, f32[8,128,128]{2,1,0:T(8,128)S(1)}, f32[8,128,128]{2,1,0:T(8,128)S(1)}, f32[4,8,128,128]{3,2,1,0:T(8,128)}, f32[4,8,128,128]{3,2,1,0:T(8,128)}, /*index=5*/s32[]{:T(128)}, s32[]{:T(128)}) while((s32[]{:T(128)}, f32[8,128,128]{2,1,0:T(8,128)S(1)}, f32[8,128,128]{2,1,0:T(8,128)S(1)}, ...), condition=%wide.region_3.4_spmd.clone, body=%wide.region_2.3_spmd.clone.sunk | while | flops 402915328 | bytes 5768791 | solution.py:267
  153.3 1.8 convolution_add_fusion.10
  157.0 1.8 convolution_add_fusion.10
  160.7 1.8 convolution_add_fusion.10
  164.4 1.8 convolution_add_fusion.10
  168.7 3.4 collective-permute-start.4
  172.3 3.6 collective-permute-start.1
  175.8 3.3 collective-permute-done.4
  179.6 5.2 collective-permute-start.5
  185.3 4.5 collective-permute-start.2
  192.0 4.8 collective-permute-start.6
  197.2 7.5 %collective-permute-start.3 = (bf16[8,128,128]{2,1,0:T(8,128)(2,1)S(1)}, bf16[8,128,128]{2,1,0:T(8,128)(2,1)S(1)}, u32[]{:S(2)}, u32[]{:S(2)}) collective-permute-start(bf16[8,128,128]{2,1,0:T(8,128)(2,1)S(1)} %get-tuple-element.273), channel_id=1, source_target_pairs={{0,8},{2,10},{4,12},{6,14},{8,16},{10,18},{12,20},{14,22},{16,24},... | collective-permute-start | bytes 786440 | tf_op jit(solution)/shard_map/ppermute | solution.py:19
  205.1 4.6 collective-permute-start.7
  209.8 2.9 fusion.43
  217.3 2.2 collective-permute-done.8
  219.5 28.7 %while.25 = (s32[]{:T(128)}, f32[8,128,128]{2,1,0:T(8,128)S(1)}, f32[4,8,64,128]{3,2,1,0:T(8,128)}, f32[4,8,128,128]{3,2,1,0:T(8,128)}, f32[4,8,128,128]{3,2,1,0...) while((s32[]{:T(128)}, f32[8,128,128]{2,1,0:T(8,128)S(1)}, ...), condition=%wide.region_6.7_spmd, body=%wide.region_5.6_spmd.sunk | while | flops 453246976 | bytes 6557285 | solution.py:175
  222.8 2.1 fusion.211
  230.0 2.1 fusion.211
  232.0 1.8 convolution_add_fusion.9
  237.2 2.1 fusion.211
  239.2 1.8 convolution_add_fusion.9
  244.3 2.1 fusion.211
  252.2 4.8 convolution_convert_fusion.2
  257.1 18.2 %reduce-scatter.3.cloned.1.call-done = bf16[128,2048]{1,0:T(8,128)(2,1)} async-done(((bf16[256,2048]{1,0:T(8,128)(2,1)}), bf16[128,2048]{1,0:T(8,128)(2,1)}) %reduce-scatter.3.cloned.1.call-update) | async-done | bytes 524304 | tf_op jit(solution)/shard_map/reduce_scatter | solution.py:277
  276.5 2.1 fusion.62
  278.7 15.5 %all-gather = s32[512,10]{1,0:T(8,128)S(1)} all-gather(s32[128,10]{1,0:T(8,128)S(1)} %copy.279), channel_id=2, replica_groups=mesh['group'=1,'ctx_hi'=4,'ctx_lo'=4,'head'=2] {'ctx_hi'}, dimensions={0}, use_global_device_ids=true | all-gather | bytes 25600 | tf_op jit(solution)/shard_map/all_gather | solution.py:294
  295.6 62.8 %reduce-window.6 = s32[4,32,10,128]{3,2,1,0:T(8,128)S(1)} reduce-window(s32[4,32,10,128]{3,2,1,0:T(8,128)} %fusion.84, s32[]{:T(128)} %constant.128.clone.1), window={size=1x1x1x128 pad=0_0x0_0x0_0x127_0}, to_apply=%region_9.10 | reduce-window | flops 20807680 | bytes 1310724 | tf_op jit(solution)/shard_map/reduce-window
  364.8 6.6 %fusion.26 = pred[512,1600]{0,1:T(8,128)(4,1)S(1)} fusion(s32[512,10]{0,1:T(8,128)S(1)} %copy.282), kind=kLoop, calls=%fused_computation.37 | loop fusion | flops 15564800 | bytes 839680 | tf_op jit(solution)/shard_map/reduce_or | solution.py:308
  371.5 5.4 convolution_convert_fusion.1
  376.8 78.5 %all_to_all.10 = bf16[8,200,2048]{2,1,0:T(8,128)(2,1)S(1)} all-to-all(bf16[8,200,2048]{2,1,0:T(8,128)(2,1)S(1)} %bitcast.295), channel_id=1, replica_groups=mesh['group'=1,'ctx_hi'=4,'ctx_lo'=4,'head'=2] {'ctx_lo','head'}, dimensions={0} | all-to-all | bytes 13107200 | tf_op jit(solution)/shard_map/all_to_all | solution.py:314
  455.3 7.1 %fusion.27 = f32[1600,1024]{1,0:T(8,128)S(1)} fusion(bf16[1600,2048]{1,0:T(8,128)(2,1)S(1)} %bitcast.296, bf16[1,2048,1024]{2,1,0:T(8,128)(2,1)S(1)} %copy-done.26), kind=kOutput, calls=%fused_computation.43 | convolution fusion | flops 6710886400 | bytes 17301504 | tf_op jit(solution)/shard_map/dot_general | solution.py:199
  462.4 5.7 convolution_convert_fusion
  468.1 4.9 all-to-all-start.1
  473.1 13.3 %all-gather.1 = f32[512,10]{0,1:T(8,128)S(1)} all-gather(f32[128,10]{0,1:T(8,128)S(1)} %copy-done.24), channel_id=3, replica_groups=mesh['group'=1,'ctx_hi'=4,'ctx_lo'=4,'head'=2] {'ctx_hi'}, dimensions={0}, use_global_device_ids=true | all-gather | bytes 25600 | tf_op jit(solution)/shard_map/all_gather | solution.py:295
  486.4 6.2 %select_reduce_fusion = f32[512,1600]{0,1:T(8,128)} fusion(f32[512,10]{0,1:T(8,128)S(1)} %all-gather.1, s32[512,10]{0,1:T(8,128)S(1)} %copy.282), kind=kLoop, calls=%fused_computation.35 | loop fusion | flops 23756800 | bytes 3317760 | tf_op jit(solution)/shard_map/reduce_sum | solution.py:327
  492.6 54.9 %all-to-all-done.1 = bf16[8,200,2048]{2,1,0:T(8,128)(2,1)} async-done(((bf16[8,200,2048]{2,1,0:T(8,128)(2,1)}), bf16[8,200,2048]{2,1,0:T(8,128)(2,1)}, u32[]{:S(2)}, u32[]{:S(2)}) %all-to-all-start.1) | async-done | bytes 6553632 | tf_op jit(solution)/shard_map/all_to_all | solution.py:325
  547.4 7.8 %fusion.91 = f32[512,2048]{1,0:T(8,128)S(1)} fusion(bf16[1600,2048]{1,0:T(8,128)(2,1)} %bitcast.73, f32[512,1600]{0,1:T(8,128)} %select_reduce_fusion), kind=kOutput, calls=%fused_computation.159 | convolution fusion | flops 3356262400 | bytes 14024704 | tf_op jit(solution)/shard_map/dot_general | solution.py:330
  555.3 8.2 %add_convert_fusion = bf16[512,2048]{1,0:T(8,128)(2,1)} fusion(f32[512,2048]{1,0:T(8,128)S(1)} %fusion.91, bf16[1600,2048]{1,0:T(8,128)(2,1)} %bitcast.73, f32[512,1600]{0,1:T(8,128)S(1)} %copy-done.1), kind=kOutput, calls=%fused_computation.46 | convolution fusion | flops 3360817152 | bytes 16121856 | tf_op jit(solution)/shard_map/dot_general | solution.py:330
  563.6 43.6 %reduce-scatter.5.cloned.1.call-done = bf16[128,2048]{1,0:T(8,128)(2,1)} async-done(((bf16[512,2048]{1,0:T(8,128)(2,1)}), bf16[128,2048]{1,0:T(8,128)(2,1)}) %reduce-scatter.5.cloned.1.call-update) | async-done | bytes 524304 | tf_op jit(solution)/shard_map/reduce_scatter | solution.py:333
  607.1 2.1 fusion.63
  (213 shorter events, 87.6 us)
Async XLA Ops:
  6.5 455.9 %copy-start = (bf16[1,512,2048]{2,1,0:T(8,128)(2,1)S(1)}, bf16[1,512,2048]{2,1,0:T(8,128)(2,1)}, u32[]{:S(2)}) copy-start(bf16[1,512,2048]{2,1,0:T(8,128)(2,1)} %param.35) | copy-start | bytes 6291460
  6.5 268.7 %reduce-scatter.3.cloned.1.call-start = ((), (), s32[]{:S(2)}) async-start(), calls=%async_computation.4 | async-start | bytes 1572864 | tf_op jit(solution)/shard_map/reduce_scatter | solution.py:277
  8.1 12.3 %collective-permute-start = (bf16[3,2048]{1,0:T(4,128)(2,1)S(1)}, bf16[3,2048]{1,0:T(4,128)(2,1)S(1)}, u32[]{:S(2)}, u32[]{:S(2)}) collective-permute-start(bf16[3,2048]{1,0:T(4,128)(2,1)S(1)} %pad_maximum_fusion), channel_id=1, source_target_pairs={{0,2},{2,4},{4,6},{6,8},{8,10},{10,12},{12,14},{14,16},{16,18},{18... | collective-permute-start | bytes 36872 | tf_op jit(solution)/shard_map/ppermute | solution.py:19
  28.6 1.0 copy-start.2
  31.7 12.7 %copy-start.6 = (f32[8,4,64,64]{3,2,1,0:T(8,128)}, f32[8,4,64,64]{3,2,1,0:T(8,128)S(1)}, u32[]{:S(2)}) copy-start(f32[8,4,64,64]{3,2,1,0:T(8,128)S(1)} %fusion.47) | copy-start | bytes 1572868
  46.8 17.8 %copy-start.21 = (f32[32,2]{1,0:T(8,128)S(1)}, f32[32,2]{1,0:T(8,128)}, u32[]{:S(2)}) copy-start(f32[32,2]{1,0:T(8,128)} %constant.141.clone.1) | copy-start | bytes 772
  66.9 19.5 %copy-start.17 = (f32[8,4,16,2,2]{4,3,2,1,0:T(2,128)}, f32[8,4,16,2,2]{4,3,2,1,0:T(2,128)S(1)}, u32[]{:S(2)}) copy-start(f32[8,4,16,2,2]{4,3,2,1,0:T(2,128)S(1)} %get-tuple-element.242) | copy-start | bytes 24580
  66.9 24.3 %copy-start.19 = (f32[8,4,16,2,2]{4,3,2,1,0:T(2,128)}, f32[8,4,16,2,2]{4,3,2,1,0:T(2,128)S(1)}, u32[]{:S(2)}) copy-start(f32[8,4,16,2,2]{4,3,2,1,0:T(2,128)S(1)} %get-tuple-element.241) | copy-start | bytes 24580
  112.2 5.7 copy-start.10
  125.1 3.9 copy-start.13
  135.7 1.2 copy-start.7
  136.6 1.6 copy-start.20
  136.6 1.7 copy-start.18
  137.6 1.3 copy-start.3
  138.5 1.9 copy-start.11
  142.4 5.3 copy-start.8
  151.7 1.5 copy-start.5
  153.3 18.9 %copy-start.25 = (f32[128]{0:T(128)S(1)}, f32[128]{0:T(128)}, u32[]{:S(2)}) copy-start(f32[128]{0:T(128)} %param.28) | copy-start | bytes 1540
  168.7 10.4 %collective-permute-start.4 = (bf16[8,128,128]{2,1,0:T(8,128)(2,1)}, bf16[8,128,128]{2,1,0:T(8,128)(2,1)S(1)}, u32[]{:S(2)}, u32[]{:S(2)}) collective-permute-start(bf16[8,128,128]{2,1,0:T(8,128)(2,1)} %convert_element_type.160), channel_id=1, source_target_pairs={{0,2},{2,4},{4,6},{6,8},{8,10},{10,12},{12,14},{14,16},{16,18},{18... | collective-permute-start | bytes 786440 | tf_op jit(solution)/shard_map/ppermute | solution.py:19
  172.3 12.6 %collective-permute-start.1 = (bf16[8,128,128]{2,1,0:T(8,128)(2,1)S(1)}, bf16[8,128,128]{2,1,0:T(8,128)(2,1)S(1)}, u32[]{:S(2)}, u32[]{:S(2)}) collective-permute-start(bf16[8,128,128]{2,1,0:T(8,128)(2,1)S(1)} %convert_element_type.157), channel_id=1, source_target_pairs={{0,2},{2,4},{4,6},{6,8},{8,10},{10,12},{12,14},{14,16},{16,18},{18... | collective-permute-start | bytes 786440 | tf_op jit(solution)/shard_map/ppermute | solution.py:19
  179.6 12.0 %collective-permute-start.5 = (bf16[8,128,128]{2,1,0:T(8,128)(2,1)S(1)}, bf16[8,128,128]{2,1,0:T(8,128)(2,1)S(1)}, u32[]{:S(2)}, u32[]{:S(2)}) collective-permute-start(bf16[8,128,128]{2,1,0:T(8,128)(2,1)S(1)} %get-tuple-element.267), channel_id=1, source_target_pairs={{0,4},{2,6},{4,8},{6,10},{8,12},{10,14},{12,16},{14,18},{16,20},{1... | collective-permute-start | bytes 786440 | tf_op jit(solution)/shard_map/ppermute | solution.py:19
  185.2 24.5 %copy-start.4 = (f32[256,4,2,128]{3,0,2,1:T(8,128)S(1)}, f32[256,4,2,128]{3,0,2,1:T(8,128)}, u32[]{:S(2)}) copy-start(f32[256,4,2,128]{3,0,2,1:T(8,128)} %copy-done.2) | copy-start | bytes 3145732
  185.3 24.5 %copy-start.12 = (f32[256,4,2,128]{3,0,2,1:T(8,128)S(1)}, f32[256,4,2,128]{3,0,2,1:T(8,128)}, u32[]{:S(2)}) copy-start(f32[256,4,2,128]{3,0,2,1:T(8,128)} %copy-done.11) | copy-start | bytes 3145732
  185.3 11.5 %collective-permute-start.2 = (bf16[8,128,128]{2,1,0:T(8,128)(2,1)S(1)}, bf16[8,128,128]{2,1,0:T(8,128)(2,1)S(1)}, u32[]{:S(2)}, u32[]{:S(2)}) collective-permute-start(bf16[8,128,128]{2,1,0:T(8,128)(2,1)S(1)} %get-tuple-element.269), channel_id=1, source_target_pairs={{0,4},{2,6},{4,8},{6,10},{8,12},{10,14},{12,16},{14,18},{16,20},{1... | collective-permute-start | bytes 786440 | tf_op jit(solution)/shard_map/ppermute | solution.py:19
  192.0 12.7 %collective-permute-start.6 = (bf16[8,128,128]{2,1,0:T(8,128)(2,1)S(1)}, bf16[8,128,128]{2,1,0:T(8,128)(2,1)S(1)}, u32[]{:S(2)}, u32[]{:S(2)}) collective-permute-start(bf16[8,128,128]{2,1,0:T(8,128)(2,1)S(1)} %get-tuple-element.271), channel_id=1, source_target_pairs={{0,8},{2,10},{4,12},{6,14},{8,16},{10,18},{12,20},{14,22},{16,24},... | collective-permute-start | bytes 786440 | tf_op jit(solution)/shard_map/ppermute | solution.py:19
  197.2 15.5 %collective-permute-start.3 = (bf16[8,128,128]{2,1,0:T(8,128)(2,1)S(1)}, bf16[8,128,128]{2,1,0:T(8,128)(2,1)S(1)}, u32[]{:S(2)}, u32[]{:S(2)}) collective-permute-start(bf16[8,128,128]{2,1,0:T(8,128)(2,1)S(1)} %get-tuple-element.273), channel_id=1, source_target_pairs={{0,8},{2,10},{4,12},{6,14},{8,16},{10,18},{12,20},{14,22},{16,24},... | collective-permute-start | bytes 786440 | tf_op jit(solution)/shard_map/ppermute | solution.py:19
  205.1 10.5 %copy-start.9 = (f32[8,4,64,256]{3,2,1,0:T(8,128)S(1)}, f32[8,4,64,256]{3,2,1,0:T(8,128)}, u32[]{:S(2)}) copy-start(f32[8,4,64,256]{3,2,1,0:T(8,128)} %copy-done.8) | copy-start | bytes 6291460
  205.1 8.5 %collective-permute-start.7 = (bf16[8,128,128]{2,1,0:T(8,128)(2,1)S(1)}, bf16[8,128,128]{2,1,0:T(8,128)(2,1)S(1)}, u32[]{:S(2)}, u32[]{:S(2)}) collective-permute-start(bf16[8,128,128]{2,1,0:T(8,128)(2,1)S(1)} %get-tuple-element.275), channel_id=1, source_target_pairs={{0,16},{2,18},{4,20},{6,22},{8,24},{10,26},{12,28},{14,30},{1,17},... | collective-permute-start | bytes 786440 | tf_op jit(solution)/shard_map/ppermute | solution.py:19
  214.1 5.4 collective-permute-start.8
  248.3 3.9 copy-start.27
  252.2 23.0 %copy-start.14 = (bf16[128,2048]{1,0:T(8,128)(2,1)S(1)}, bf16[128,2048]{1,0:T(8,128)(2,1)}, u32[]{:S(2)}) copy-start(bf16[128,2048]{1,0:T(8,128)(2,1)} %param.30) | copy-start | bytes 1572868
  252.2 24.3 %copy-start.22 = (f32[2048]{0:T(1024)S(1)}, f32[2048]{0:T(1024)}, u32[]{:S(2)}) copy-start(f32[2048]{0:T(1024)} %param.31) | copy-start | bytes 24580
  257.0 21.6 %copy-start.23 = (s32[128,10]{0,1:T(8,128)S(1)}, s32[128,10]{0,1:T(8,128)}, u32[]{:S(2)}) copy-start(s32[128,10]{0,1:T(8,128)} %param.32) | copy-start | bytes 15364
  257.0 114.4 %all-gather.5.cloned.1.call-start = ((), (), s32[]{:S(2)}) async-start(), calls=%async_computation.6 | async-start | bytes 2621440 | tf_op jit(solution)/shard_map/all_gather | solution.py:293
  376.8 78.5 %copy-start.26 = (bf16[1,2048,1024]{2,1,0:T(8,128)(2,1)S(1)}, bf16[1,2048,1024]{2,1,0:T(8,128)(2,1)}, u32[]{:S(2)}) copy-start(bf16[1,2048,1024]{2,1,0:T(8,128)(2,1)} %param.34) | copy-start | bytes 12582916
  468.1 5.0 copy-start.24
  468.1 79.3 %all-to-all-start.1 = ((bf16[8,200,2048]{2,1,0:T(8,128)(2,1)}), bf16[8,200,2048]{2,1,0:T(8,128)(2,1)}, u32[]{:S(2)}, u32[]{:S(2)}) async-start(bf16[8,200,2048]{2,1,0:T(8,128)(2,1)} %bitcast.294), calls=%async_computation.2 | async-start | bytes 13107200 | tf_op jit(solution)/shard_map/all_to_all | solution.py:325
  473.0 134.1 %reduce-scatter.5.cloned.1.call-start = ((), (), s32[]{:S(2)}) async-start(), calls=%async_computation.5 | async-start | bytes 2621440 | tf_op jit(solution)/shard_map/reduce_scatter | solution.py:333
  547.4 7.8 %copy-start.1 = (f32[512,1600]{0,1:T(8,128)S(1)}, f32[512,1600]{0,1:T(8,128)}, u32[]{:S(2)}) copy-start(f32[512,1600]{0,1:T(8,128)} %select_reduce_fusion) | copy-start | bytes 9830404
  555.3 51.9 %copy-start.15 = (bf16[128,2048]{1,0:T(8,128)(2,1)S(1)}, bf16[128,2048]{1,0:T(8,128)(2,1)}, u32[]{:S(2)}) copy-start(bf16[128,2048]{1,0:T(8,128)(2,1)} %param.30) | copy-start | bytes 1572868
  555.3 51.8 %copy-start.16 = (bf16[128,2048]{1,0:T(8,128)(2,1)S(1)}, bf16[128,2048]{1,0:T(8,128)(2,1)}, u32[]{:S(2)}) copy-start(bf16[128,2048]{1,0:T(8,128)(2,1)} %reduce-scatter.3.cloned.1.call-done) | copy-start | bytes 1572868
Sparse Core Ops, SparseCore 0:
  257.1 18.0 reduce-scatter.2
  278.7 48.0 all-gather.4
  563.7 43.3 reduce-scatter.4

commit v3 on v2

--- a/solution.py
+++ b/solution.py
@@ -290,12 +290,39 @@
     local_rows = routes.shape[0]
     top_count = routes.shape[1]
     capacity = local_rows * top_count * 5 // (4 * experts_all)
-    gathered_in = lax.all_gather(expert_in, "ctx_hi").reshape(levels * local_rows, D)
-    gathered_routes = lax.all_gather(routes, "ctx_hi").reshape(levels, local_rows * top_count)
-    gathered_weights = lax.all_gather(route_weights, "ctx_hi").reshape(levels * local_rows, top_count)
+    own_high = route_weights.astype(jnp.bfloat16)
+    own_low = (route_weights - own_high.astype(jnp.float32)).astype(jnp.bfloat16)
+    spare = -(-(3 * top_count) // 128) * 128 - 3 * top_count
+    packed = jnp.concatenate(
+        [
+            expert_in,
+            routes.astype(jnp.bfloat16),
+            own_high,
+            own_low,
+            jnp.zeros((local_rows, spare), jnp.bfloat16),
+        ],
+        axis=1,
+    )
+    gathered = lax.all_gather(packed, "ctx_hi").reshape(levels * local_rows, -1)
+    gathered_in = gathered[:, :D]
+    gathered_routes = gathered[:, D : D + top_count].astype(jnp.int32)
+    gathered_high = gathered[:, D + top_count : D + 2 * top_count]
+    gathered_low = gathered[:, D + 2 * top_count : D + 3 * top_count]
     expert_ids = jnp.arange(experts_all, dtype=jnp.int32)
-    onehot = (gathered_routes[:, :, None] == expert_ids[None, None, :]).astype(jnp.int32)
-    slot_rank = jnp.sum((jnp.cumsum(onehot, axis=1) - 1) * onehot, axis=2)
+    row_hot = jnp.any(gathered_routes[:, :, None] == expert_ids[None, None, :], axis=1)
+    row_hot = row_hot.reshape(levels, local_rows, experts_all).astype(jnp.bfloat16)
+    earlier_rows = (
+        lax.broadcasted_iota(jnp.int32, (local_rows, local_rows), 0)
+        > lax.broadcasted_iota(jnp.int32, (local_rows, local_rows), 1)
+    ).astype(jnp.bfloat16)
+    earlier = jnp.einsum(
+        "ij,sje->sie", earlier_rows, row_hot, preferred_element_type=jnp.float32
+    ).reshape(levels * local_rows, 1, experts_all)
+    slot_rank = jnp.sum(
+        jnp.where(gathered_routes[:, :, None] == expert_ids[None, None, :], earlier, 0.0), axis=2
+    ).astype(jnp.int32)
+    gathered_routes = gathered_routes.reshape(levels, local_rows * top_count)
+    slot_rank = slot_rank.reshape(levels, local_rows * top_count)
     source = lax.broadcasted_iota(jnp.int32, gathered_routes.shape, 0)
     within = gathered_routes % per_level
     slot_index = jnp.where(
@@ -324,9 +351,12 @@
     ).reshape(per_level // local_experts, local_experts * levels * capacity, D)
     returned = lax.all_to_all(answered, level_axes, split_axis=0, concat_axis=0, tiled=True)
     result_rows = returned.reshape(slots_total, D)
-    weight_table = jnp.sum(jnp.where(hits, gathered_weights[:, :, None], 0.0), axis=1)
-    weight_high = weight_table.astype(jnp.bfloat16)
-    weight_low = (weight_table - weight_high.astype(jnp.float32)).astype(jnp.bfloat16)
+    weight_high = jnp.sum(jnp.where(hits, gathered_high[:, :, None], 0.0), axis=1).astype(
+        jnp.bfloat16
+    )
+    weight_low = jnp.sum(jnp.where(hits, gathered_low[:, :, None], 0.0), axis=1).astype(
+        jnp.bfloat16
+    )
     partial = jnp.dot(weight_high, result_rows, preferred_element_type=jnp.float32) + jnp.dot(
         weight_low, result_rows, preferred_element_type=jnp.float32
     )

time: 628 us -> 587 us (0.935)
  other arithmetic: 102 us -> 37.3 us
  waiting for transfers between devices: 125 us -> 181 us
  blocking collectives: 107 us -> 78.2 us
    another operation x2 -> x0, other arithmetic: 62.8 us -> none
    all_gather x1, waiting for transfers between devices: 0.02 us -> 49.6 us  [per_device(): gathered = lax.all_gather(packed, 'ctx_hi').reshape(levels * local_rows, -1)]
    all_gather x2 -> x0, blocking collectives: 28.8 us -> none  [the longest x1 15.5 us: per_device(): lax.all_gather(routes, 'ctx_hi').reshape(levels, local_rows * top_count)]
    all_to_all x1, waiting for transfers between devices: 54.9 us -> 65.3 us  [per_device(): lax.all_to_all(answered, level_axes, split_axis=0, concat_axis=0, tiled=T...]
  transfers between devices with their start and end apart: 13 -> 13, of which waited for: 7 -> 8; matrix products, arithmetic and copies ran while one was open for 16% -> 4% of each run, Pallas kernels for 0% -> 0%
where the time goes in v3:
time: 587 us; the launch traced here: 579 us
  waiting for transfers between devices  181 us (31%)
  matrix products  117 us (20%)
  local copies, waits for them, and re-layouts  105 us (18%)
  blocking collectives  78.2 us (13%)
  starting transfers between devices  45.5 us (8%)
  other arithmetic  37.3 us (6%)
  between operations  14.5 us (2%)
    all_to_all x1, blocking collectives, per_device(): lax.all_to_all(outgoing, level_axes, split_axis=0, concat_axis=0, tiled=T...  78.2 us
    all_to_all x1, waiting for transfers between devices, per_device(): lax.all_to_all(answered, level_axes, split_axis=0, concat_axis=0, tiled=T...  65.3 us
    all_gather x1, waiting for transfers between devices, per_device(): gathered = lax.all_gather(packed, 'ctx_hi').reshape(levels * local_rows, -1)  49.6 us
    reshape x8, local copies, waits for them, and re-layouts, unit_lower_inverse(): grid = system.reshape(lead + (count, 2 * width, count, 2 * width))  46.5 us
    dot_general x31, matrix products, batched(): return jnp.einsum('hij,hjk->hik', left, right, precision=HIGHEST)  45.4 us
    reduce_scatter x1, waiting for transfers between devices, per_device(): lax.psum_scatter(partial.astype(jnp.bfloat16), 'ctx_hi', scatter_dimensio...  41.1 us
    ppermute x9, starting transfers between devices, passed_along(): return lax.ppermute(block, axis, route)  40.1 us
    gather x9, local copies, waits for them, and re-layouts, unit_lower_inverse(): diagonal = jnp.moveaxis(jnp.diagonal(grid, axis1=-4, axis2=-2), -1, -3)  24.4 us
  transfers between devices with their start and end apart: 13, of which 8 were waited for; matrix products, arithmetic and copies ran while one was open for 4% of the time, Pallas kernels for 0%

profile of v3, /device:TPU:0, one launch (start us, length us, event | category | flops | bytes accessed | tf_op | source)
XLA Modules:
  0.0 578.7 jit_solution(49206661583943542)
XLA Ops:
  8.1 4.8 collective-permute-start
  20.8 2.9 multiply_bitcast_fusion.1
  28.6 2.0 fusion.52
  30.6 4.6 copy.310
  35.3 4.6 reshape.297
  39.8 3.7 reshape.298
  43.6 2.5 reshape.299
  46.1 12.1 %copy.392 = f32[8,4,32,2,32,2]{0,1,4,2,5,3:T(4,128)} copy(f32[8,4,32,2,32,2]{0,5,4,3,2,1:T(2,128)} %bitcast.290) | data formatting | bytes 1048576 | tf_op jit(solution)/shard_map/vmap(vmap())/reshape | solution.py:85
  58.2 4.1 gather_fusion
  65.8 10.8 %copy.391 = f32[8,4,16,4,16,4]{0,5,4,2,3,1:T(4,128)} copy(f32[8,4,16,4,16,4]{0,5,4,3,2,1:T(4,128)} %bitcast.291) | data formatting | bytes 1048576 | tf_op jit(solution)/shard_map/vmap(vmap())/reshape | solution.py:85
  76.6 5.1 gather_fusion.1
  81.7 3.6 copy.316
  85.3 4.8 fusion.112
  90.1 4.0 convolution_negate_fusion.4
  94.0 1.9 select_maximum_fusion.4
  96.0 8.7 %copy.390 = f32[8,4,8,8,8,8]{5,3,4,2,1,0:T(8,128)} copy(f32[8,4,8,8,8,8]{5,4,3,2,1,0:T(8,128)} %reshape.297) | data formatting | bytes 1048576 | tf_op jit(solution)/shard_map/vmap(vmap())/reshape | solution.py:85
  104.7 5.0 gather_fusion.2
  114.2 2.6 convolution_negate_fusion.3
  116.8 2.5 copy.393
  119.3 2.8 gather_fusion.3
  129.4 2.2 gather_fusion.4
  140.3 2.0 fusion.35
  142.3 3.8 convolution_bitcast_fusion
  147.6 4.0 bitcast_subtract_fusion
  153.2 14.7 %while.26 = (s32[]{:T(128)}, f32[8,128,128]{2,1,0:T(8,128)S(1)}, f32[8,128,128]{2,1,0:T(8,128)S(1)}, f32[4,8,128,128]{3,2,1,0:T(8,128)}, f32[4,8,128,128]{3,2,1,0:T(8,128)}, /*index=5*/s32[]{:T(128)}, s32[]{:T(128)}) while((s32[]{:T(128)}, f32[8,128,128]{2,1,0:T(8,128)S(1)}, f32[8,128,128]{2,1,0:T(8,128)S(1)}, ...), condition=%wide.region_3.4_spmd.clone, body=%wide.region_2.3_spmd.clone.sunk | while | flops 402915328 | bytes 5768791 | solution.py:267
  153.2 1.8 convolution_add_fusion.10
  156.9 1.8 convolution_add_fusion.10
  160.6 1.8 convolution_add_fusion.10
  164.3 1.8 convolution_add_fusion.10
  168.6 3.4 collective-permute-start.4
  172.2 3.6 collective-permute-start.1
  175.8 3.3 collective-permute-done.4
  179.5 5.2 collective-permute-start.5
  185.1 4.3 collective-permute-start.2
  189.5 2.0 collective-permute-done.5
  191.9 5.1 collective-permute-start.6
  197.4 7.0 %collective-permute-start.3 = (bf16[8,128,128]{2,1,0:T(8,128)(2,1)S(1)}, bf16[8,128,128]{2,1,0:T(8,128)(2,1)S(1)}, u32[]{:S(2)}, u32[]{:S(2)}) collective-permute-start(bf16[8,128,128]{2,1,0:T(8,128)(2,1)S(1)} %get-tuple-element.294), channel_id=1, source_target_pairs={{0,8},{2,10},{4,12},{6,14},{8,16},{10,18},{12,20},{14,22},{16,24},... | collective-permute-start | bytes 786440 | tf_op jit(solution)/shard_map/ppermute | solution.py:19
  204.9 4.4 collective-permute-start.7
  209.3 2.9 fusion.48
  213.6 2.1 collective-permute-start.8
  217.4 2.2 collective-permute-done.8
  219.6 28.7 %while.25 = (s32[]{:T(128)}, f32[8,128,128]{2,1,0:T(8,128)S(1)}, f32[4,8,64,128]{3,2,1,0:T(8,128)}, f32[4,8,128,128]{3,2,1,0:T(8,128)}, f32[4,8,128,128]{3,2,1,0...) while((s32[]{:T(128)}, f32[8,128,128]{2,1,0:T(8,128)S(1)}, ...), condition=%wide.region_6.7_spmd, body=%wide.region_5.6_spmd.sunk | while | flops 453246976 | bytes 6557285 | solution.py:175
  222.9 2.1 fusion.218
  224.9 1.8 convolution_add_fusion.9
  230.0 2.1 fusion.218
  232.1 1.8 convolution_add_fusion.9
  237.2 2.0 fusion.218
  244.4 2.1 fusion.218
  246.4 1.8 convolution_add_fusion.9
  252.3 4.7 convolution_convert_fusion.2
  257.9 17.3 %reduce-scatter.3.cloned.1.call-done = bf16[128,2048]{1,0:T(8,128)(2,1)} async-done(((bf16[256,2048]{1,0:T(8,128)(2,1)}), bf16[128,2048]{1,0:T(8,128)(2,1)}) %reduce-scatter.3.cloned.1.call-update) | async-done | bytes 524304 | tf_op jit(solution)/shard_map/reduce_scatter | solution.py:277
  278.8 49.6 %all-gather.3.cloned.1.call-done = bf16[512,2176]{1,0:T(8,128)(2,1)} async-done(((bf16[128,2176]{1,0:T(8,128)(2,1)}), bf16[512,2176]{1,0:T(8,128)(2,1)}) %all-gather.3.cloned.1.call-update) | async-done | bytes 2228240 | tf_op jit(solution)/shard_map/all_gather | solution.py:306
  331.7 6.6 %fusion.27 = pred[512,1600]{0,1:T(8,128)(4,1)S(1)} fusion(s32[512,10]{0,1:T(8,128)S(1)} %copy.346), kind=kLoop, calls=%fused_computation.37 | loop fusion | flops 15564800 | bytes 839680 | tf_op jit(solution)/shard_map/reduce_or | solution.py:335
  338.3 5.4 convolution_convert_fusion.1
  343.6 78.2 %all_to_all.10 = bf16[8,200,2048]{2,1,0:T(8,128)(2,1)S(1)} all-to-all(bf16[8,200,2048]{2,1,0:T(8,128)(2,1)S(1)} %bitcast.305), channel_id=1, replica_groups=mesh['group'=1,'ctx_hi'=4,'ctx_lo'=4,'head'=2] {'ctx_lo','head'}, dimensions={0} | all-to-all | bytes 13107200 | tf_op jit(solution)/shard_map/all_to_all | solution.py:341
  421.9 7.2 %fusion.31 = f32[1600,1024]{1,0:T(8,128)S(1)} fusion(bf16[1600,2048]{1,0:T(8,128)(2,1)S(1)} %bitcast.306, bf16[1,2048,1024]{2,1,0:T(8,128)(2,1)S(1)} %copy-done.33), kind=kOutput, calls=%fused_computation.46 | convolution fusion | flops 6710886400 | bytes 17301504 | tf_op jit(solution)/shard_map/dot_general | solution.py:199
  429.1 5.7 convolution_convert_fusion
  434.8 4.8 all-to-all-start.1
  440.0 8.6 %fusion.30 = (bf16[512,1600]{0,1:T(8,128)(2,1)}, bf16[512,1600]{0,1:T(8,128)(2,1)}) fusion(s32[512,10]{0,1:T(8,128)S(1)} %copy.346, bf16[512,10]{0,1:T(8,128)(2,1)S(1)} %copy.348, bf16[512,10]{0,1:T(8,128)(2,1)S(1)} %copy.347), kind=kLoop, calls=%fused_computation.40 | loop fusion | flops 39321600 | bytes 3317760 | tf_op jit(solution)/shard_map/reduce_sum | solution.py:357
  448.7 65.3 %all-to-all-done.1 = bf16[8,200,2048]{2,1,0:T(8,128)(2,1)} async-done(((bf16[8,200,2048]{2,1,0:T(8,128)(2,1)}), bf16[8,200,2048]{2,1,0:T(8,128)(2,1)}, u32[]{:S(2)}, u32[]{:S(2)}) %all-to-all-start.1) | async-done | bytes 6553632 | tf_op jit(solution)/shard_map/all_to_all | solution.py:352
  513.9 6.7 %fusion.156 = f32[512,2048]{1,0:T(8,128)S(1)} fusion(bf16[512,1600]{0,1:T(8,128)(2,1)} %get-tuple-element.216, bf16[1600,2048]{1,0:T(8,128)(2,1)} %bitcast.73), kind=kOutput, calls=%fused_computation.276 | convolution fusion | flops 3355443200 | bytes 12386304 | tf_op jit(solution)/shard_map/dot_general | solution.py:360
  520.7 8.1 %add_convert_fusion = bf16[512,2048]{1,0:T(8,128)(2,1)} fusion(f32[512,2048]{1,0:T(8,128)S(1)} %fusion.156, bf16[512,1600]{0,1:T(8,128)(2,1)S(1)} %copy-done.10, bf16[1600,2048]{1,0:T(8,128)(2,1)} %bitcast.73), kind=kOutput, calls=%fused_computation.49 | convolution fusion | flops 3357540352 | bytes 14483456 | tf_op jit(solution)/shard_map/dot_general | solution.py:360
  528.8 41.1 %reduce-scatter.5.cloned.1.call-done = bf16[128,2048]{1,0:T(8,128)(2,1)} async-done(((bf16[512,2048]{1,0:T(8,128)(2,1)}), bf16[128,2048]{1,0:T(8,128)(2,1)}) %reduce-scatter.5.cloned.1.call-update) | async-done | bytes 524304 | tf_op jit(solution)/shard_map/reduce_scatter | solution.py:363
  569.9 2.1 fusion.68
  (228 shorter events, 80.5 us)
Async XLA Ops:
  6.5 422.6 %copy-start = (bf16[1,512,2048]{2,1,0:T(8,128)(2,1)S(1)}, bf16[1,512,2048]{2,1,0:T(8,128)(2,1)}, u32[]{:S(2)}) copy-start(bf16[1,512,2048]{2,1,0:T(8,128)(2,1)} %param.35) | copy-start | bytes 6291460
  6.5 13.9 %copy-start.27 = (bf16[256,1024]{1,0:T(8,128)(2,1)S(1)}, bf16[256,1024]{1,0:T(8,128)(2,1)}, u32[]{:S(2)}) copy-start(bf16[256,1024]{1,0:T(8,128)(2,1)} %param.21) | copy-start | bytes 1572868
  6.5 268.7 %reduce-scatter.3.cloned.1.call-start = ((), (), s32[]{:S(2)}) async-start(), calls=%async_computation.4 | async-start | bytes 1572864 | tf_op jit(solution)/shard_map/reduce_scatter | solution.py:277
  8.1 12.3 %collective-permute-start = (bf16[3,2048]{1,0:T(4,128)(2,1)S(1)}, bf16[3,2048]{1,0:T(4,128)(2,1)S(1)}, u32[]{:S(2)}, u32[]{:S(2)}) collective-permute-start(bf16[3,2048]{1,0:T(4,128)(2,1)S(1)} %pad_maximum_fusion), channel_id=1, source_target_pairs={{0,2},{2,4},{4,6},{6,8},{8,10},{10,12},{12,14},{14,16},{16,18},{18... | collective-permute-start | bytes 36872 | tf_op jit(solution)/shard_map/ppermute | solution.py:19
  27.6 1.0 copy-start.1
  30.6 13.0 %copy-start.5 = (f32[8,4,64,64]{3,2,1,0:T(8,128)}, f32[8,4,64,64]{3,2,1,0:T(8,128)S(1)}, u32[]{:S(2)}) copy-start(f32[8,4,64,64]{3,2,1,0:T(8,128)S(1)} %fusion.52) | copy-start | bytes 1572868
  46.1 17.4 %copy-start.28 = (f32[32,2]{1,0:T(8,128)S(1)}, f32[32,2]{1,0:T(8,128)}, u32[]{:S(2)}) copy-start(f32[32,2]{1,0:T(8,128)} %constant.139.clone.1) | copy-start | bytes 772
  65.8 19.5 %copy-start.16 = (f32[8,4,16,2,2]{4,3,2,1,0:T(2,128)}, f32[8,4,16,2,2]{4,3,2,1,0:T(2,128)S(1)}, u32[]{:S(2)}) copy-start(f32[8,4,16,2,2]{4,3,2,1,0:T(2,128)S(1)} %get-tuple-element.263) | copy-start | bytes 24580
  65.8 24.2 %copy-start.21 = (f32[8,4,16,2,2]{4,3,2,1,0:T(2,128)}, f32[8,4,16,2,2]{4,3,2,1,0:T(2,128)S(1)}, u32[]{:S(2)}) copy-start(f32[8,4,16,2,2]{4,3,2,1,0:T(2,128)S(1)} %get-tuple-element.262) | copy-start | bytes 24580
  90.1 4.0 copy-start.17
  111.1 5.7 copy-start.9
  122.1 1.0 copy-start.19
  122.1 1.2 copy-start.22
  122.1 1.3 copy-start.23
  123.9 3.9 copy-start.13
  131.6 1.0 copy-start.20
  131.6 1.2 copy-start.24
  131.6 1.3 copy-start.25
  134.8 1.2 copy-start.6
  135.1 2.3 copy-start.26
  135.2 2.3 copy-start.18
  137.4 1.4 copy-start.2
  137.6 2.7 copy-start.11
  142.3 5.3 copy-start.7
  151.6 1.6 copy-start.4
  153.1 19.0 %copy-start.32 = (f32[128]{0:T(128)S(1)}, f32[128]{0:T(128)}, u32[]{:S(2)}) copy-start(f32[128]{0:T(128)} %param.28) | copy-start | bytes 1540
  168.6 10.5 %collective-permute-start.4 = (bf16[8,128,128]{2,1,0:T(8,128)(2,1)}, bf16[8,128,128]{2,1,0:T(8,128)(2,1)S(1)}, u32[]{:S(2)}, u32[]{:S(2)}) collective-permute-start(bf16[8,128,128]{2,1,0:T(8,128)(2,1)} %convert_element_type.176), channel_id=1, source_target_pairs={{0,2},{2,4},{4,6},{6,8},{8,10},{10,12},{12,14},{14,16},{16,18},{18... | collective-permute-start | bytes 786440 | tf_op jit(solution)/shard_map/ppermute | solution.py:19
  172.2 12.6 %collective-permute-start.1 = (bf16[8,128,128]{2,1,0:T(8,128)(2,1)S(1)}, bf16[8,128,128]{2,1,0:T(8,128)(2,1)S(1)}, u32[]{:S(2)}, u32[]{:S(2)}) collective-permute-start(bf16[8,128,128]{2,1,0:T(8,128)(2,1)S(1)} %convert_element_type.173), channel_id=1, source_target_pairs={{0,2},{2,4},{4,6},{6,8},{8,10},{10,12},{12,14},{14,16},{16,18},{18... | collective-permute-start | bytes 786440 | tf_op jit(solution)/shard_map/ppermute | solution.py:19
  179.5 12.0 %collective-permute-start.5 = (bf16[8,128,128]{2,1,0:T(8,128)(2,1)S(1)}, bf16[8,128,128]{2,1,0:T(8,128)(2,1)S(1)}, u32[]{:S(2)}, u32[]{:S(2)}) collective-permute-start(bf16[8,128,128]{2,1,0:T(8,128)(2,1)S(1)} %get-tuple-element.288), channel_id=1, source_target_pairs={{0,4},{2,6},{4,8},{6,10},{8,12},{10,14},{12,16},{14,18},{16,20},{1... | collective-permute-start | bytes 786440 | tf_op jit(solution)/shard_map/ppermute | solution.py:19
  185.1 11.8 %collective-permute-start.2 = (bf16[8,128,128]{2,1,0:T(8,128)(2,1)S(1)}, bf16[8,128,128]{2,1,0:T(8,128)(2,1)S(1)}, u32[]{:S(2)}, u32[]{:S(2)}) collective-permute-start(bf16[8,128,128]{2,1,0:T(8,128)(2,1)S(1)} %get-tuple-element.290), channel_id=1, source_target_pairs={{0,4},{2,6},{4,8},{6,10},{8,12},{10,14},{12,16},{14,18},{16,20},{1... | collective-permute-start | bytes 786440 | tf_op jit(solution)/shard_map/ppermute | solution.py:19
  191.9 17.4 %copy-start.3 = (f32[256,4,2,128]{3,0,2,1:T(8,128)S(1)}, f32[256,4,2,128]{3,0,2,1:T(8,128)}, u32[]{:S(2)}) copy-start(f32[256,4,2,128]{3,0,2,1:T(8,128)} %copy-done.1) | copy-start | bytes 3145732
  191.9 17.4 %copy-start.12 = (f32[256,4,2,128]{3,0,2,1:T(8,128)S(1)}, f32[256,4,2,128]{3,0,2,1:T(8,128)}, u32[]{:S(2)}) copy-start(f32[256,4,2,128]{3,0,2,1:T(8,128)} %copy-done.11) | copy-start | bytes 3145732
  191.9 12.5 %collective-permute-start.6 = (bf16[8,128,128]{2,1,0:T(8,128)(2,1)S(1)}, bf16[8,128,128]{2,1,0:T(8,128)(2,1)S(1)}, u32[]{:S(2)}, u32[]{:S(2)}) collective-permute-start(bf16[8,128,128]{2,1,0:T(8,128)(2,1)S(1)} %get-tuple-element.292), channel_id=1, source_target_pairs={{0,8},{2,10},{4,12},{6,14},{8,16},{10,18},{12,20},{14,22},{16,24},... | collective-permute-start | bytes 786440 | tf_op jit(solution)/shard_map/ppermute | solution.py:19
  197.4 14.9 %collective-permute-start.3 = (bf16[8,128,128]{2,1,0:T(8,128)(2,1)S(1)}, bf16[8,128,128]{2,1,0:T(8,128)(2,1)S(1)}, u32[]{:S(2)}, u32[]{:S(2)}) collective-permute-start(bf16[8,128,128]{2,1,0:T(8,128)(2,1)S(1)} %get-tuple-element.294), channel_id=1, source_target_pairs={{0,8},{2,10},{4,12},{6,14},{8,16},{10,18},{12,20},{14,22},{16,24},... | collective-permute-start | bytes 786440 | tf_op jit(solution)/shard_map/ppermute | solution.py:19
  204.9 8.3 %collective-permute-start.7 = (bf16[8,128,128]{2,1,0:T(8,128)(2,1)S(1)}, bf16[8,128,128]{2,1,0:T(8,128)(2,1)S(1)}, u32[]{:S(2)}, u32[]{:S(2)}) collective-permute-start(bf16[8,128,128]{2,1,0:T(8,128)(2,1)S(1)} %get-tuple-element.296), channel_id=1, source_target_pairs={{0,16},{2,18},{4,20},{6,22},{8,24},{10,26},{12,28},{14,30},{1,17},... | collective-permute-start | bytes 786440 | tf_op jit(solution)/shard_map/ppermute | solution.py:19
  212.2 3.5 copy-start.8
  213.6 6.0 %collective-permute-start.8 = (bf16[8,128,128]{2,1,0:T(8,128)(2,1)S(1)}, bf16[8,128,128]{2,1,0:T(8,128)(2,1)S(1)}, u32[]{:S(2)}, u32[]{:S(2)}) collective-permute-start(bf16[8,128,128]{2,1,0:T(8,128)(2,1)S(1)} %fusion.60), channel_id=1, source_target_pairs={{0,2},{2,4},{4,6},{6,8},{8,10},{10,12},{12,14},{14,16},{16,18},{18... | collective-permute-start | bytes 786440 | tf_op jit(solution)/shard_map/ppermute | solution.py:19
  248.3 3.9 copy-start.34
  252.2 5.3 copy-start.31
  252.2 5.5 copy-start.30
  252.3 23.0 %copy-start.14 = (bf16[128,2048]{1,0:T(8,128)(2,1)S(1)}, bf16[128,2048]{1,0:T(8,128)(2,1)}, u32[]{:S(2)}) copy-start(bf16[128,2048]{1,0:T(8,128)(2,1)} %param.30) | copy-start | bytes 1572868
  257.0 19.5 %copy-start.29 = (f32[2048]{0:T(1024)S(1)}, f32[2048]{0:T(1024)}, u32[]{:S(2)}) copy-start(f32[2048]{0:T(1024)} %param.31) | copy-start | bytes 24580
  257.0 71.4 %all-gather.3.cloned.1.call-start = ((), (), s32[]{:S(2)}) async-start(), calls=%async_computation.6 | async-start | bytes 2785280 | tf_op jit(solution)/shard_map/all_gather | solution.py:306
  343.6 78.3 %copy-start.33 = (bf16[1,2048,1024]{2,1,0:T(8,128)(2,1)S(1)}, bf16[1,2048,1024]{2,1,0:T(8,128)(2,1)}, u32[]{:S(2)}) copy-start(bf16[1,2048,1024]{2,1,0:T(8,128)(2,1)} %param.34) | copy-start | bytes 12582916
  434.8 79.2 %all-to-all-start.1 = ((bf16[8,200,2048]{2,1,0:T(8,128)(2,1)}), bf16[8,200,2048]{2,1,0:T(8,128)(2,1)}, u32[]{:S(2)}, u32[]{:S(2)}) async-start(bf16[8,200,2048]{2,1,0:T(8,128)(2,1)} %bitcast.304), calls=%async_computation.2 | async-start | bytes 13107200 | tf_op jit(solution)/shard_map/all_to_all | solution.py:352
  439.5 130.4 %reduce-scatter.5.cloned.1.call-start = ((), (), s32[]{:S(2)}) async-start(), calls=%async_computation.5 | async-start | bytes 2621440 | tf_op jit(solution)/shard_map/reduce_scatter | solution.py:363
  513.9 6.7 %copy-start.10 = (bf16[512,1600]{0,1:T(8,128)(2,1)S(1)}, bf16[512,1600]{0,1:T(8,128)(2,1)}, u32[]{:S(2)}) copy-start(bf16[512,1600]{0,1:T(8,128)(2,1)} %get-tuple-element.215) | copy-start | bytes 4915204
  528.8 41.1 %copy-start.15 = (bf16[128,2048]{1,0:T(8,128)(2,1)S(1)}, bf16[128,2048]{1,0:T(8,128)(2,1)}, u32[]{:S(2)}) copy-start(bf16[128,2048]{1,0:T(8,128)(2,1)} %reduce-scatter.3.cloned.1.call-done) | copy-start | bytes 1572868
Sparse Core Ops, SparseCore 0:
  257.1 18.0 reduce-scatter.2
  278.9 49.4 all-gather.2
  529.0 40.8 reduce-scatter.4
